TPU v7x, 128 devices: a whole 4x4x4 slice. The times are simulated.
128 devices in a mesh: dp: 16 (over y, z_hi, core), mp: 8 (over x, z_lo).
Axes of the slice: x: 4, y: 4, z: 4 (z_hi: 2, z_lo: 2; z = z_hi * 2 + z_lo), core: 2. Of those that a mesh axis runs over, the one named last changes fastest.
Arguments:
- features: bfloat16 [8192, 8192], P('mp', 'dp'), may hold values from -6 to 6
- cotangent: bfloat16 [8192, 8192], P('mp', 'dp'), may hold values from -6 to 6
- block_perm: int32 [16, 512], P('mp'), may hold values from 0 to 511, each once within a row
- w_gate: bfloat16 [16, 512, 2048], P('mp'), may hold values from -0.25 to 0.25
- w_up: bfloat16 [16, 512, 2048], P('mp'), may hold values from -0.25 to 0.25
- w_down: bfloat16 [16, 2048, 512], P('mp'), may hold values from -0.125 to 0.125
Outputs:
- outputs: bfloat16 [8192, 8192], P('mp', 'dp')
- d_features: bfloat16 [8192, 8192], P('mp', 'dp')
- gate_grad: float32 [16, 512, 2048], P('mp', 'dp')
- up_grad: float32 [16, 512, 2048], P('mp', 'dp')
- down_grad: float32 [16, 2048, 512], P('mp', 'dp')
Inputs may be any that keep to these rules, and one draw needn't show every extreme that they name: Each row of block_perm names every number below 512 exactly once.
All inputs are finite; a program needn't handle non-finite values.
Results may differ from a plain program's by a relative error of at most 0.012.
Values may be sent and summed in bfloat16 or wider, within the bound.
No kernel may reach another device: no remote copies, remote signals or barrier semaphores. Data moves between devices by JAX's collectives and lax.ppermute only.
A program may use at most 128 MiB of HBM per device.

v0:
```python
import jax
import jax.numpy as jnp
from jax import lax
from jax.sharding import PartitionSpec as P

input_scale = 2.0
output_scale = 0.5


def inverse_rows(block_perm):
    count = block_perm.shape[1]
    targets = lax.broadcasted_iota(jnp.int32, (1, 1, count), 2)
    places = lax.broadcasted_iota(jnp.int32, (1, count, 1), 1)
    match = block_perm[:, :, None] == targets
    return jnp.sum(jnp.where(match, places, 0), axis=1)


def local(features, cotangent, block_perm, w_gate, w_up, w_down):
    tok_count = features.shape[1]
    blocks_here = w_gate.shape[0]
    inner = w_gate.shape[1]
    hidden_width = w_gate.shape[2]
    block_total = blocks_here * lax.axis_size("mp")
    piece = inner // block_total
    grad_scale = (tok_count * lax.axis_size("dp")) ** (-0.5)
    local_shape = (blocks_here, block_total, piece, tok_count)
    feat_local = features.reshape(local_shape)
    cot_local = cotangent.reshape(local_shape)
    feat_blocks, cot_blocks = (
        lax.all_to_all(feat_local, "mp", split_axis=1, concat_axis=0, tiled=True),
        lax.all_to_all(cot_local, "mp", split_axis=1, concat_axis=0, tiled=True),
    )
    inverse = inverse_rows(block_perm)
    gate_rows = jnp.take_along_axis(w_gate, inverse[:, :, None], axis=1).reshape(
        blocks_here, block_total, piece, hidden_width
    )
    up_rows = jnp.take_along_axis(w_up, inverse[:, :, None], axis=1).reshape(
        blocks_here, block_total, piece, hidden_width
    )
    gate = (
        jnp.einsum("sbkt,bskh->bth", feat_blocks, gate_rows, preferred_element_type=jnp.float32)
        * input_scale
    )
    up = (
        jnp.einsum("sbkt,bskh->bth", feat_blocks, up_rows, preferred_element_type=jnp.float32)
        * input_scale
    )
    sig = jax.nn.sigmoid(gate)
    act = gate * sig
    hidden = (act * up).astype(jnp.bfloat16)
    down_view = w_down.reshape(blocks_here, hidden_width, block_total, piece)
    mixed = (
        jnp.einsum("bth,bhsk->sbkt", hidden, down_view, preferred_element_type=jnp.float32)
        * output_scale
    ).astype(jnp.bfloat16)
    outputs = lax.all_to_all(mixed, "mp", split_axis=0, concat_axis=1, tiled=True).reshape(
        features.shape
    )
    down_part = (
        jnp.einsum("bth,sbkt->bhsk", hidden, cot_blocks, preferred_element_type=jnp.float32)
        * (output_scale * grad_scale)
    ).reshape(blocks_here, hidden_width, inner)
    d_hidden = (
        jnp.einsum("sbkt,bhsk->bth", cot_blocks, down_view, preferred_element_type=jnp.float32)
        * output_scale
    )
    d_gate = (d_hidden * up * (sig * (1.0 + gate * (1.0 - sig)))).astype(jnp.bfloat16)
    d_up = (d_hidden * act).astype(jnp.bfloat16)
    d_mixed = (
        (
            jnp.einsum("bth,bskh->sbkt", d_gate, gate_rows, preferred_element_type=jnp.float32)
            + jnp.einsum("bth,bskh->sbkt", d_up, up_rows, preferred_element_type=jnp.float32)
        )
        * input_scale
    ).astype(jnp.bfloat16)
    d_features = lax.all_to_all(d_mixed, "mp", split_axis=0, concat_axis=1, tiled=True).reshape(
        features.shape
    )
    gate_part = (
        jnp.einsum("sbkt,bth->bskh", feat_blocks, d_gate, preferred_element_type=jnp.float32)
        * (input_scale * grad_scale)
    ).reshape(blocks_here, inner, hidden_width)
    up_part = (
        jnp.einsum("sbkt,bth->bskh", feat_blocks, d_up, preferred_element_type=jnp.float32)
        * (input_scale * grad_scale)
    ).reshape(blocks_here, inner, hidden_width)
    gate_part = jnp.take_along_axis(gate_part, block_perm[:, :, None], axis=1)
    up_part = jnp.take_along_axis(up_part, block_perm[:, :, None], axis=1)
    gate_grad, up_grad, down_grad = (
        lax.psum_scatter(
            gate_part.astype(jnp.bfloat16), "dp", scatter_dimension=1, tiled=True
        ).astype(jnp.float32),
        lax.psum_scatter(
            up_part.astype(jnp.bfloat16), "dp", scatter_dimension=1, tiled=True
        ).astype(jnp.float32),
        lax.psum_scatter(
            down_part.astype(jnp.bfloat16), "dp", scatter_dimension=1, tiled=True
        ).astype(jnp.float32),
    )
    return (outputs, d_features, gate_grad, up_grad, down_grad)


def solution(mesh):
    placed = (
        P("mp", "dp"),
        P("mp", "dp"),
        P("mp", None),
        P("mp", None, None),
        P("mp", None, None),
        P("mp", None, None),
    )
    return jax.shard_map(
        local,
        mesh=mesh,
        in_specs=placed,
        out_specs=(
            P("mp", "dp"),
            P("mp", "dp"),
            P("mp", "dp", None),
            P("mp", "dp", None),
            P("mp", "dp", None),
        ),
        check_vma=False,
    )
```

profile of v0, /device:TPU:0, one launch (start us, length us, event | category | flops | bytes accessed | tf_op | source)
XLA Modules:
  0.0 465.1 jit_solution(10760179304425741431)
XLA Ops:
  7.2 2.4 copy.72
  9.6 5.8 %all-to-all-start = ((bf16[2,16,32,512]{3,2,0,1:T(8,128)(2,1)}), bf16[2,16,32,512]{3,2,0,1:T(8,128)(2,1)S(1)}, u32[]{:S(2)}, u32[]{:S(2)}) async-start(bf16[2,16,32,512]{3,2,0,1:T(8,128)(2,1)} %copy.72), calls=%async_computation | async-start | bytes 2097152 | tf_op jit(solution)/shard_map/all_to_all | solution.py:30
  15.3 1.0 copy.79
  16.4 0.3 select_reduce_fusion
  16.7 14.5 %all-to-all-done = bf16[2,16,32,512]{3,2,0,1:T(8,128)(2,1)S(1)} async-done(((bf16[2,16,32,512]{3,2,0,1:T(8,128)(2,1)}), bf16[2,16,32,512]{3,2,0,1:T(8,128)(2,1)S(1)}, u32[]{:S(2)}, u32[]{:S(2)}) %all-to-all-start) | async-done | bytes 1048608 | tf_op jit(solution)/shard_map/all_to_all | solution.py:30
  31.3 3.6 all-to-all-start.2
  34.8 0.0 reduce-scatter.4.cloned.1.call-start
  34.9 25.5 %gather_fusion.1 = bf16[1024,2048]{1,0:T(8,128)(2,1)} fusion(bf16[2,512,2048]{2,1,0:T(8,128)(2,1)} %param.14, s32[1024]{0:T(1024)S(1)} %bitcast.167), kind=kCustom, calls=%fused_computation.2.clone | custom fusion | bytes 8396800 | tf_op jit(solution)/shard_map/jit(take_along_axis)/gather | solution.py:37
  60.4 25.4 %gather_fusion = bf16[1024,2048]{1,0:T(8,128)(2,1)} fusion(bf16[2,512,2048]{2,1,0:T(8,128)(2,1)} %param.13, s32[1024]{0:T(1024)S(1)} %bitcast.168), kind=kCustom, calls=%fused_computation.clone | custom fusion | bytes 8396800 | tf_op jit(solution)/shard_map/jit(take_along_axis)/gather | solution.py:34
  85.8 6.2 %copy.75 = bf16[2,2048,512]{1,2,0:T(8,128)(2,1)} copy(bf16[2,2048,512]{2,1,0:T(8,128)(2,1)} %param.15) | data formatting | bytes 8388608 | tf_op args[5]
  92.1 5.9 %broadcast_select_fusion.1 = (bf16[2,512,2048]{2,1,0:T(8,128)(2,1)}, bf16[2,512,2048]{2,1,0:T(8,128)(2,1)}) fusion(bf16[2,512,2048]{2,1,0:T(8,128)(2,1)} %bitcast.172, pred[2,512]{1,0:T(4,128)(4,1)S(1)} %and_bitcast_fusion.1, bf16[2,512,2048]{2,1,0:T(8,128)(2,1)} %bitcast.171), kind=kLoop, calls=%fused_computation.34 | loop fusion | flops 4194304 | bytes 16778240 | tf_op jit(solution)/shard_map/jit(take_along_axis)/select_n | solution.py:34
  98.0 0.1 copy.74
  98.1 0.0 all-to-all-done.2
  98.1 0.1 copy.81
  98.2 8.0 %fusion.25 = f32[2,2048,512,1]{2,1,3,0:T(8,128)} fusion(bf16[2,16,32,2048]{3,2,1,0:T(8,128)(2,1)} %bitcast.176, bf16[16,2,32,512]{3,2,0,1:T(8,128)(2,1)S(1)} %bitcast.192), kind=kOutput, calls=%fused_computation.48 | convolution fusion | flops 2147483648 | bytes 13631488 | tf_op jit(solution)/shard_map/sbkt,bskh->bth/dot_general | solution.py:41
  106.2 2.4 fusion.26
  108.6 14.4 %fusion.2 = (bf16[2,512,2048]{1,2,0:T(8,128)(2,1)}, bf16[2,512,2048,1]{1,2,3,0:T(8,128)(2,1)}, bf16[2,512,2048]{1,2,0:T(8,128)(2,1)}) fusion(f32[2,2048,512,1]{2,1,3,0:T(8,128)} %fusion.25, f32[2,512,2048,1]{1,2,3,0:T(8,128)S(1)} %fusion.26, bf16[2,16,32,2048]{3,2,1,0:T(8,128)(2,1)} %bitcast.178, bf16[16,2,32,512]{3,2,0,1:T(8,128)(2,1)S(1)} %bitcast.193), kind=kOutput, calls=%fused_computation.9 | convolution fusion | flops 2185232384 | bytes 34603008 | tf_op jit(solution)/shard_map/sbkt,bskh->bth/dot_general | solution.py:45
  123.0 6.8 %broadcast_multiply_fusion.1 = bf16[2,2048,16,32]{1,3,2,0:T(8,128)(2,1)} fusion(bf16[16,2,32,512]{3,2,0,1:T(8,128)(2,1)S(1)} %bitcast.194, bf16[2,512,2048]{1,2,0:T(8,128)(2,1)} %get-tuple-element.7), kind=kOutput, calls=%fused_computation.32 | convolution fusion | flops 2151677952 | bytes 9437184 | tf_op jit(solution)/shard_map/sbkt,bth->bskh/dot_general | solution.py:80
  129.8 4.4 broadcast_multiply_fusion
  134.2 25.5 %gather_fusion.2 = bf16[1024,2048]{1,0:T(8,128)(2,1)} fusion(bf16[2,512,2048]{2,1,0:T(8,128)(2,1)} %bitcast.170, s32[1024]{0:T(1024)S(1)} %bitcast.165), kind=kCustom, calls=%fused_computation.1.clone | custom fusion | bytes 8396800 | tf_op jit(solution)/shard_map/jit(take_along_axis)/gather | solution.py:87
  159.7 25.5 %gather_fusion.3 = bf16[1024,2048]{1,0:T(8,128)(2,1)} fusion(bf16[2,512,2048]{2,1,0:T(8,128)(2,1)} %bitcast.169, s32[1024]{0:T(1024)S(1)} %bitcast.166), kind=kCustom, calls=%fused_computation.3.clone | custom fusion | bytes 8396800 | tf_op jit(solution)/shard_map/jit(take_along_axis)/gather | solution.py:88
  185.2 7.2 %select_convert_fusion = (bf16[2,512,2048]{2,1,0:T(8,128)(2,1)}, bf16[2,512,2048]{2,1,0:T(8,128)(2,1)}) fusion(bf16[2,512,2048]{2,1,0:T(8,128)(2,1)} %bitcast.174, pred[2,512]{1,0:T(4,128)(4,1)S(1)} %and_bitcast_fusion, bf16[2,512,2048]{2,1,0:T(8,128)(2,1)} %bitcast.173), kind=kLoop, calls=%fused_computation.20 | loop fusion | flops 4194304 | bytes 16778240 | tf_op jit(solution)/shard_map/convert_element_type | solution.py:94
  192.4 0.0 reduce-scatter.4.cloned.1.call-update
  192.5 0.0 reduce-scatter.6.cloned.1.call-start
  192.5 0.7 reduce-scatter.6.cloned.1.call-update
  193.2 0.0 reduce-scatter.8.cloned.1.call-start
  193.3 6.7 %multiply_convert_fusion = bf16[2,2048,16,32]{1,3,2,0:T(8,128)(2,1)} fusion(bf16[16,2,32,512]{3,2,0,1:T(8,128)(2,1)S(1)} %bitcast.186, bf16[2,512,2048]{1,2,0:T(8,128)(2,1)} %get-tuple-element.9), kind=kOutput, calls=%fused_computation.22 | convolution fusion | flops 2151677952 | bytes 9437184 | tf_op jit(solution)/shard_map/bth,sbkt->bhsk/dot_general | solution.py:60
  200.0 6.4 %copy.90 = bf16[2,2048,512]{2,1,0:T(8,128)(2,1)} copy(bf16[2,2048,512]{1,2,0:T(8,128)(2,1)} %bitcast.180) | data formatting | bytes 8388608 | tf_op jit(solution)/shard_map/convert_element_type | solution.py:97
  206.4 0.0 reduce-scatter.8.cloned.1.call-update
  206.5 6.4 %fusion.27 = f32[2,16,32,512]{3,2,1,0:T(8,128)S(1)} fusion(bf16[2,16,32,2048]{3,2,1,0:T(8,128)(2,1)} %bitcast.179, bf16[2,512,2048,1]{1,2,3,0:T(8,128)(2,1)} %get-tuple-element.8), kind=kOutput, calls=%fused_computation.50 | convolution fusion | flops 2147483648 | bytes 10485760 | tf_op jit(solution)/shard_map/bth,bskh->sbkt/dot_general | solution.py:72
  212.8 0.4 copy-done.4
  213.2 2.3 fusion.21
  215.6 1.0 copy.85
  216.6 5.5 %all-to-all-start.3 = ((bf16[16,2,32,512]{3,2,1,0:T(8,128)(2,1)}), bf16[16,2,32,512]{3,2,1,0:T(8,128)(2,1)S(1)}, u32[]{:S(2)}, u32[]{:S(2)}) async-start(bf16[16,2,32,512]{3,2,1,0:T(8,128)(2,1)} %copy.85), calls=%async_computation.3 | async-start | bytes 2097152 | tf_op jit(solution)/shard_map/all_to_all | solution.py:76
  222.1 5.8 %fusion.28 = f32[2,512,512]{1,2,0:S(1)} fusion(bf16[2,2048,512]{2,1,0:T(8,128)(2,1)} %param.15, bf16[2,512,2048]{1,2,0:T(8,128)(2,1)} %get-tuple-element.9), kind=kOutput, calls=%fused_computation.51 | convolution fusion | flops 2147483648 | bytes 10485760
  228.0 0.3 fusion.24
  228.3 1.0 copy.77
  229.3 7.9 %all-to-all-done.3 = bf16[16,2,32,512]{3,2,1,0:T(8,128)(2,1)S(1)} async-done(((bf16[16,2,32,512]{3,2,1,0:T(8,128)(2,1)}), bf16[16,2,32,512]{3,2,1,0:T(8,128)(2,1)S(1)}, u32[]{:S(2)}, u32[]{:S(2)}) %all-to-all-start.3) | async-done | bytes 1048608 | tf_op jit(solution)/shard_map/all_to_all | solution.py:76
  237.2 3.6 all-to-all-start.1
  240.8 1.0 copy.86
  241.8 16.2 %all-to-all-done.1 = bf16[16,2,32,512]{3,2,1,0:T(8,128)(2,1)S(1)} async-done(((bf16[16,2,32,512]{3,2,1,0:T(8,128)(2,1)}), bf16[16,2,32,512]{3,2,1,0:T(8,128)(2,1)S(1)}, u32[]{:S(2)}, u32[]{:S(2)}) %all-to-all-start.1) | async-done | bytes 1048608 | tf_op jit(solution)/shard_map/all_to_all | solution.py:56
  258.0 1.0 copy.78
  259.1 30.8 %reduce-scatter.4.cloned.1.call-done = bf16[2,32,2048]{2,1,0:T(8,128)(2,1)} async-done(((bf16[2,512,2048]{2,1,0:T(8,128)(2,1)}), bf16[2,32,2048]{2,1,0:T(8,128)(2,1)}) %reduce-scatter.4.cloned.1.call-update) | async-done | bytes 262160 | tf_op jit(solution)/shard_map/reduce_scatter | solution.py:90
  289.9 1.8 convert_element_type.50
  291.7 81.7 %reduce-scatter.6.cloned.1.call-done = bf16[2,32,2048]{2,1,0:T(8,128)(2,1)} async-done(((bf16[2,512,2048]{2,1,0:T(8,128)(2,1)}), bf16[2,32,2048]{2,1,0:T(8,128)(2,1)}) %reduce-scatter.6.cloned.1.call-update) | async-done | bytes 262160 | tf_op jit(solution)/shard_map/reduce_scatter | solution.py:93
  373.3 1.8 convert_element_type.52
  375.1 81.7 %reduce-scatter.8.cloned.1.call-done = bf16[2,128,512]{2,1,0:T(8,128)(2,1)} async-done(((bf16[2,2048,512]{2,1,0:T(8,128)(2,1)}), bf16[2,128,512]{2,1,0:T(8,128)(2,1)}) %reduce-scatter.8.cloned.1.call-update) | async-done | bytes 262160 | tf_op jit(solution)/shard_map/reduce_scatter | solution.py:96
  456.8 1.8 convert_element_type.55
  (17 shorter events, 0.1 us)
Async XLA Ops:
  7.2 8.2 %copy-start.2 = (bf16[1024,512]{1,0:T(8,128)(2,1)S(1)}, bf16[1024,512]{1,0:T(8,128)(2,1)}, u32[]{:S(2)}) copy-start(bf16[1024,512]{1,0:T(8,128)(2,1)} %param.11) | copy-start | bytes 3145732
  7.2 9.2 %copy-start.3 = (s32[2,512]{1,0:T(2,128)S(1)}, s32[2,512]{1,0:T(2,128)}, u32[]{:S(2)}) copy-start(s32[2,512]{1,0:T(2,128)} %param.12) | copy-start | bytes 12292
  9.6 21.7 %all-to-all-start = ((bf16[2,16,32,512]{3,2,0,1:T(8,128)(2,1)}), bf16[2,16,32,512]{3,2,0,1:T(8,128)(2,1)S(1)}, u32[]{:S(2)}, u32[]{:S(2)}) async-start(bf16[2,16,32,512]{3,2,0,1:T(8,128)(2,1)} %copy.72), calls=%async_computation | async-start | bytes 2097152 | tf_op jit(solution)/shard_map/all_to_all | solution.py:30
  31.3 66.8 %all-to-all-start.2 = ((bf16[2,16,32,512]{3,2,0,1:T(8,128)(2,1)}), bf16[2,16,32,512]{3,2,0,1:T(8,128)(2,1)S(1)}, u32[]{:S(2)}, u32[]{:S(2)}) async-start(bf16[2,16,32,512]{3,2,0,1:T(8,128)(2,1)} %copy.79), calls=%async_computation.2 | async-start | bytes 2097152 | tf_op jit(solution)/shard_map/all_to_all | solution.py:31
  34.8 255.1 %reduce-scatter.4.cloned.1.call-start = ((), (), s32[]{:S(2)}) async-start(), calls=%async_computation.7 | async-start | bytes 4456448 | tf_op jit(solution)/shard_map/reduce_scatter | solution.py:90
  98.2 8.0 %copy-start = (bf16[2,2048,512]{1,2,0:T(8,128)(2,1)S(1)}, bf16[2,2048,512]{1,2,0:T(8,128)(2,1)}, u32[]{:S(2)}) copy-start(bf16[2,2048,512]{1,2,0:T(8,128)(2,1)} %copy.75) | copy-start | bytes 12582916
  123.0 6.8 %copy-start.5 = (bf16[2,512,2048,1]{1,2,3,0:T(8,128)(2,1)S(1)}, bf16[2,512,2048,1]{1,2,3,0:T(8,128)(2,1)}, u32[]{:S(2)}) copy-start(bf16[2,512,2048,1]{1,2,3,0:T(8,128)(2,1)} %get-tuple-element.8) | copy-start | bytes 12582916
  192.5 180.9 %reduce-scatter.6.cloned.1.call-start = ((), (), s32[]{:S(2)}) async-start(), calls=%async_computation.8 | async-start | bytes 4456448 | tf_op jit(solution)/shard_map/reduce_scatter | solution.py:93
  193.2 263.6 %reduce-scatter.8.cloned.1.call-start = ((), (), s32[]{:S(2)}) async-start(), calls=%async_computation.9 | async-start | bytes 4456448 | tf_op jit(solution)/shard_map/reduce_scatter | solution.py:96
  206.4 6.4 %copy-start.1 = (bf16[2,512,2048]{2,1,0:T(8,128)(2,1)S(1)}, bf16[2,512,2048]{2,1,0:T(8,128)(2,1)}, u32[]{:S(2)}) copy-start(bf16[2,512,2048]{2,1,0:T(8,128)(2,1)} %get-tuple-element.12) | copy-start | bytes 12582916
  206.5 6.8 %copy-start.4 = (bf16[2,512,2048]{1,2,0:T(8,128)(2,1)S(1)}, bf16[2,512,2048]{1,2,0:T(8,128)(2,1)}, u32[]{:S(2)}) copy-start(bf16[2,512,2048]{1,2,0:T(8,128)(2,1)} %get-tuple-element.7) | copy-start | bytes 12582916
  216.6 20.6 %all-to-all-start.3 = ((bf16[16,2,32,512]{3,2,1,0:T(8,128)(2,1)}), bf16[16,2,32,512]{3,2,1,0:T(8,128)(2,1)S(1)}, u32[]{:S(2)}, u32[]{:S(2)}) async-start(bf16[16,2,32,512]{3,2,1,0:T(8,128)(2,1)} %copy.85), calls=%async_computation.3 | async-start | bytes 2097152 | tf_op jit(solution)/shard_map/all_to_all | solution.py:76
  237.2 20.8 %all-to-all-start.1 = ((bf16[16,2,32,512]{3,2,1,0:T(8,128)(2,1)}), bf16[16,2,32,512]{3,2,1,0:T(8,128)(2,1)S(1)}, u32[]{:S(2)}, u32[]{:S(2)}) async-start(bf16[16,2,32,512]{3,2,1,0:T(8,128)(2,1)} %copy.77), calls=%async_computation.1 | async-start | bytes 2097152 | tf_op jit(solution)/shard_map/all_to_all | solution.py:56
Sparse Core Ops, SparseCore 0:
  192.6 97.2 reduce-scatter.3
  293.9 79.3 reduce-scatter.5
  377.4 79.3 reduce-scatter.7
where the time goes:
time: 468 us; the launch traced here: 465 us
  waiting for transfers between devices  234 us (50%)
  local copies, waits for them, and re-layouts  123 us (26%)
  matrix products  57.2 us (12%)
  other arithmetic  19.1 us (4%)
  starting transfers between devices  18.6 us (4%)
  between operations  13.9 us (3%)
    reduce_scatter x1, waiting for transfers between devices, local(): lax.psum_scatter(up_part.astype(jnp.bfloat16), 'dp', scatter_dimension=1,...  81.7 us
    reduce_scatter x1, waiting for transfers between devices, local(): lax.psum_scatter(down_part.astype(jnp.bfloat16), 'dp', scatter_dimension=...  81.7 us
    reduce_scatter x1, waiting for transfers between devices, local(): lax.psum_scatter(gate_part.astype(jnp.bfloat16), 'dp', scatter_dimension=...  30.8 us
    gather x1, local copies, waits for them, and re-layouts, local(): gate_part = jnp.take_along_axis(gate_part, block_perm[:, :, None], axis=1)  25.5 us
    gather x1, local copies, waits for them, and re-layouts, local(): jnp.take_along_axis(w_up, inverse[:, :, None], axis=1)  25.5 us
    gather x1, local copies, waits for them, and re-layouts, local(): up_part = jnp.take_along_axis(up_part, block_perm[:, :, None], axis=1)  25.5 us
    gather x1, local copies, waits for them, and re-layouts, local(): jnp.take_along_axis(w_gate, inverse[:, :, None], axis=1)  25.4 us
    all_to_all x1, waiting for transfers between devices, local(): lax.all_to_all(mixed, 'mp', split_axis=0, concat_axis=1, tiled=True)  16.2 us
  transfers between devices with their start and end apart: 7, of which 6 were waited for; matrix products, arithmetic and copies ran while one was open for 22% of the time, Pallas kernels for 0%

commit v1 on v0

v1 whole, which is shorter than its diff:
```python
import jax
import jax.numpy as jnp
from jax import lax
from jax.sharding import PartitionSpec as P

input_scale = 2.0
output_scale = 0.5


def perm_matrix(block_perm):
    count = block_perm.shape[1]
    targets = lax.broadcasted_iota(jnp.int32, (1, 1, count), 2)
    return (block_perm[:, :, None] == targets).astype(jnp.bfloat16)


def local(features, cotangent, block_perm, w_gate, w_up, w_down):
    tok_count = features.shape[1]
    blocks_here = w_gate.shape[0]
    inner = w_gate.shape[1]
    hidden_width = w_gate.shape[2]
    n_mp = lax.axis_size("mp")
    n_dp = lax.axis_size("dp")
    block_total = blocks_here * n_mp
    piece = inner // block_total
    s_here = features.shape[0] // (block_total * piece)
    grad_scale = (tok_count * n_dp) ** (-0.5)

    both = jnp.stack([features, cotangent]).reshape(2, s_here, block_total, piece, tok_count)
    both = lax.all_to_all(both, "mp", split_axis=2, concat_axis=1, tiled=True)
    feat_blocks = both[0]
    cot_blocks = both[1]

    onehot = perm_matrix(block_perm)
    feat_rows = feat_blocks.transpose(1, 0, 2, 3).reshape(blocks_here, inner, tok_count)
    feat_p = jnp.einsum(
        "bij,bjt->bit", onehot, feat_rows, preferred_element_type=jnp.float32
    ).astype(jnp.bfloat16)

    gate = (
        jnp.einsum("bit,bih->bth", feat_p, w_gate, preferred_element_type=jnp.float32)
        * input_scale
    )
    up = (
        jnp.einsum("bit,bih->bth", feat_p, w_up, preferred_element_type=jnp.float32)
        * input_scale
    )
    sig = jax.nn.sigmoid(gate)
    act = gate * sig
    hidden = (act * up).astype(jnp.bfloat16)
    down_view = w_down.reshape(blocks_here, hidden_width, block_total, piece)

    chunk = n_dp
    down_part = (
        jnp.einsum("bth,sbkt->bhsk", hidden, cot_blocks, preferred_element_type=jnp.float32)
        * (output_scale * grad_scale)
    ).astype(jnp.bfloat16)
    down_grad = lax.psum_scatter(
        down_part.reshape(blocks_here, hidden_width, inner), "dp", scatter_dimension=1, tiled=True
    ).astype(jnp.float32)

    mixed = (
        jnp.einsum("bth,bhsk->sbkt", hidden, down_view, preferred_element_type=jnp.float32)
        * output_scale
    ).astype(jnp.bfloat16)

    d_hidden = (
        jnp.einsum("sbkt,bhsk->bth", cot_blocks, down_view, preferred_element_type=jnp.float32)
        * output_scale
    )
    d_gate = (d_hidden * up * (sig * (1.0 + gate * (1.0 - sig)))).astype(jnp.bfloat16)
    d_up = (d_hidden * act).astype(jnp.bfloat16)

    gate_part = (
        jnp.einsum("bit,bth->bih", feat_p, d_gate, preferred_element_type=jnp.float32)
        * (input_scale * grad_scale)
    ).astype(jnp.bfloat16)
    up_part = (
        jnp.einsum("bit,bth->bih", feat_p, d_up, preferred_element_type=jnp.float32)
        * (input_scale * grad_scale)
    ).astype(jnp.bfloat16)
    gate_grad = lax.psum_scatter(gate_part, "dp", scatter_dimension=1, tiled=True).astype(
        jnp.float32
    )
    up_grad = lax.psum_scatter(up_part, "dp", scatter_dimension=1, tiled=True).astype(
        jnp.float32
    )

    d_mixed_p = (
        (
            jnp.einsum("bth,bih->bit", d_gate, w_gate, preferred_element_type=jnp.float32)
            + jnp.einsum("bth,bih->bit", d_up, w_up, preferred_element_type=jnp.float32)
        )
        * input_scale
    ).astype(jnp.bfloat16)
    d_mixed = jnp.einsum(
        "bij,bit->bjt", onehot, d_mixed_p, preferred_element_type=jnp.float32
    ).astype(jnp.bfloat16)
    d_mixed = d_mixed.reshape(blocks_here, block_total, piece, tok_count).transpose(1, 0, 2, 3)

    back = jnp.stack([mixed, d_mixed])
    back = lax.all_to_all(back, "mp", split_axis=1, concat_axis=2, tiled=True)
    outputs = back[0].reshape(features.shape)
    d_features = back[1].reshape(features.shape)
    del chunk
    return (outputs, d_features, gate_grad, up_grad, down_grad)


def solution(mesh):
    placed = (
        P("mp", "dp"),
        P("mp", "dp"),
        P("mp", None),
        P("mp", None, None),
        P("mp", None, None),
        P("mp", None, None),
    )
    return jax.shard_map(
        local,
        mesh=mesh,
        in_specs=placed,
        out_specs=(
            P("mp", "dp"),
            P("mp", "dp"),
            P("mp", "dp", None),
            P("mp", "dp", None),
            P("mp", "dp", None),
        ),
        check_vma=False,
    )
```

time: 468 us -> 363 us (0.78)
  local copies, waits for them, and re-layouts: 123 us -> 18.6 us
  blocking collectives: 0 us -> 32.9 us
  starting transfers between devices: 18.6 us -> 5.89 us
  other arithmetic: 19.1 us -> 7.57 us
  waiting for transfers between devices: 234 us -> 224 us
    gather x4 -> x0, local copies, waits for them, and re-layouts: 102 us -> none  [the longest x1 25.5 us: local(): gate_part = jnp.take_along_axis(gate_part, block_perm[:, :, None], axis=1)]
    all_to_all x0 -> x1, blocking collectives: none -> 32.9 us  [local(): back = lax.all_to_all(back, 'mp', split_axis=1, concat_axis=2, tiled=True)]
    all_to_all x4 -> x1, waiting for transfers between devices: 38.6 us -> 24.9 us  [local(): both = lax.all_to_all(both, 'mp', split_axis=2, concat_axis=1, tiled=True)]
    all_to_all x4 -> x1, starting transfers between devices: 18.5 us -> 5.77 us  [local(): both = lax.all_to_all(both, 'mp', split_axis=2, concat_axis=1, tiled=True)]
    convert_element_type x3 -> x0, local copies, waits for them, and re-layouts: 8.5 us -> none  [the longest x1 6.42 us: local(): down_part.astype(jnp.bfloat16)]
    convert_element_type x5 -> x3, other arithmetic: 12.9 us -> 5.35 us  [the longest x1 1.8 us: local(): down_grad = lax.psum_scatter(down_part.reshape(blocks_here, hidden_width,...]
    select_n x1 -> x0, other arithmetic: 5.9 us -> none  [local(): jnp.take_along_axis(w_gate, inverse[:, :, None], axis=1)]
    reduce_scatter x3, waiting for transfers between devices: 194 us -> 199 us  [the longest x1 81.7 us: local(): lax.psum_scatter(gate_part, 'dp', scatter_dimension=1, tiled=True)]
  transfers between devices with their start and end apart: 7 -> 4, of which waited for: 6 -> 4; matrix products, arithmetic and copies ran while one was open for 22% -> 12% of each run, Pallas kernels for 0% -> 0%
where the time goes in v1:
time: 363 us; the launch traced here: 362 us
  waiting for transfers between devices  224 us (62%)
  matrix products  58.9 us (16%)
  blocking collectives  32.9 us (9%)
  local copies, waits for them, and re-layouts  18.6 us (5%)
  between operations  13.9 us (4%)
  other arithmetic  7.57 us (2%)
  starting transfers between devices  5.89 us (2%)
    reduce_scatter x1, waiting for transfers between devices, local(): lax.psum_scatter(gate_part, 'dp', scatter_dimension=1, tiled=True)  81.7 us
    reduce_scatter x1, waiting for transfers between devices, local(): lax.psum_scatter(up_part, 'dp', scatter_dimension=1, tiled=True)  81.7 us
    reduce_scatter x1, waiting for transfers between devices, local(): lax.psum_scatter(down_part.reshape(blocks_here, hidden_width, inner), 'dp...  36 us
    all_to_all x1, blocking collectives, local(): back = lax.all_to_all(back, 'mp', split_axis=1, concat_axis=2, tiled=True)  32.9 us
    all_to_all x1, waiting for transfers between devices, local(): both = lax.all_to_all(both, 'mp', split_axis=2, concat_axis=1, tiled=True)  24.9 us
    dot_general x1, matrix products, local(): jnp.einsum('bit,bih->bth', feat_p, w_up, preferred_element_type=jnp.float32)  13.4 us
    unnamed x11, local copies, waits for them, and re-layouts  7.46 us
  transfers between devices with their start and end apart: 4, of which 4 were waited for; matrix products, arithmetic and copies ran while one was open for 12% of the time, Pallas kernels for 0%

profile of v1, /device:TPU:0, one launch (start us, length us, event | category | flops | bytes accessed | tf_op | source)
XLA Modules:
  0.0 362.0 jit_solution(14012123323188646270)
XLA Ops:
  7.2 1.7 pad_maximum_fusion
  8.9 1.6 copy.49
  10.5 5.8 %all-to-all-start = ((bf16[2,2,16,32,512]{4,3,1,0,2:T(8,128)(2,1)}), bf16[2,2,16,32,512]{4,3,1,0,2:T(8,128)(2,1)S(1)}, u32[]{:S(2)}, u32[]{:S(2)}) async-start(bf16[2,2,16,32,512]{4,3,1,0,2:T(8,128)(2,1)} %copy.49), calls=%async_computation | async-start | bytes 4194304 | tf_op jit(solution)/shard_map/all_to_all | solution.py:29
  16.2 0.0 reduce-scatter.8.cloned.1.call-start
  16.3 6.3 %copy.56 = bf16[2,2048,512]{1,2,0:T(8,128)(2,1)} copy(bf16[2,2048,512]{2,1,0:T(8,128)(2,1)} %param.11) | data formatting | bytes 8388608 | tf_op args[5]
  22.6 24.9 %all-to-all-done = bf16[2,2,16,32,512]{4,3,1,0,2:T(8,128)(2,1)S(1)} async-done(((bf16[2,2,16,32,512]{4,3,1,0,2:T(8,128)(2,1)}), bf16[2,2,16,32,512]{4,3,1,0,2:T(8,128)(2,1)S(1)}, u32[]{:S(2)}, u32[]{:S(2)}) %all-to-all-start) | async-done | bytes 2097184 | tf_op jit(solution)/shard_map/all_to_all | solution.py:29
  47.5 0.2 copy.50
  47.7 0.2 fusion.14
  47.9 0.0 copy-start.3
  47.9 0.0 copy-start
  47.9 0.1 copy.51
  48.1 0.1 copy.52
  48.1 0.1 copy.57
  48.2 0.4 copy-done.3
  48.6 0.8 fusion.7
  49.4 0.8 copy-done
  50.1 5.6 %fusion.17 = f32[2,512,2048,1]{2,1,3,0:T(8,128)} fusion(bf16[16,2,32,512]{3,2,0,1:T(8,128)(2,1)S(1)} %bitcast.69, bf16[2,2048,16,32]{1,3,2,0:T(8,128)(2,1)S(1)} %bitcast.63), kind=kOutput, calls=%fused_computation.28 | convolution fusion | flops 2147483648 | bytes 13631488 | tf_op jit(solution)/shard_map/sbkt,bhsk->bth/dot_general | solution.py:67
  55.7 0.0 copy-done.1
  55.7 2.4 fusion.15
  58.1 13.4 %multiply_convert_fusion.5 = (bf16[2,512,2048]{2,1,0:T(8,128)(2,1)}, bf16[2,512,2048]{2,1,0:T(8,128)(2,1)}, bf16[2,512,2048]{2,1,0:T(8,128)(2,1)}) fusion(f32[2,512,2048]{2,1,0:T(8,128)S(1)} %fusion.15, f32[2,512,2048,1]{2,1,3,0:T(8,128)} %fusion.17, bf16[2,512,512]{2,1,0:T(8,128)(2,1)S(1)} %fusion.7, bf16[2,512,2048]{2,1,0:T(8,128)(2,1)} %param.10), kind=kOutput, calls=%fused_computation.6 | convolution fusion | flops 2185232384 | bytes 34603008 | tf_op jit(solution)/shard_map/bit,bih->bth/dot_general | solution.py:44
  71.5 6.5 %multiply_convert_fusion = bf16[2,2048,16,32]{1,3,2,0:T(8,128)(2,1)} fusion(bf16[16,2,32,512]{3,2,0,1:T(8,128)(2,1)S(1)} %bitcast.70, bf16[2,512,2048]{2,1,0:T(8,128)(2,1)} %get-tuple-element.5), kind=kOutput, calls=%fused_computation.1 | convolution fusion | flops 2151677952 | bytes 9437184 | tf_op jit(solution)/shard_map/bth,sbkt->bhsk/dot_general | solution.py:54
  78.0 6.2 %copy.61 = bf16[2,2048,512]{2,1,0:T(8,128)(2,1)} copy(bf16[2,2048,512]{1,2,0:T(8,128)(2,1)} %bitcast.64) | data formatting | bytes 8388608 | tf_op jit(solution)/shard_map/reshape | solution.py:58
  84.2 0.0 reduce-scatter.8.cloned.1.call-update
  84.2 0.0 reduce-scatter.6.cloned.1.call-start
  84.3 6.5 %multiply_convert_fusion.1 = bf16[2,512,2048]{2,1,0:T(8,128)(2,1)} fusion(bf16[2,512,512]{2,1,0:T(8,128)(2,1)S(1)} %fusion.7, bf16[2,512,2048]{2,1,0:T(8,128)(2,1)} %get-tuple-element.7), kind=kOutput, calls=%fused_computation.2 | convolution fusion | flops 2151677952 | bytes 9437184 | tf_op jit(solution)/shard_map/bit,bth->bih/dot_general | solution.py:78
  90.8 0.0 reduce-scatter.6.cloned.1.call-update
  90.8 0.0 reduce-scatter.4.cloned.1.call-start
  90.9 6.7 %multiply_convert_fusion.2 = bf16[2,512,2048]{2,1,0:T(8,128)(2,1)} fusion(bf16[2,512,512]{2,1,0:T(8,128)(2,1)S(1)} %fusion.7, bf16[2,512,2048]{2,1,0:T(8,128)(2,1)} %get-tuple-element.6), kind=kOutput, calls=%fused_computation.3 | convolution fusion | flops 2151677952 | bytes 9437184 | tf_op jit(solution)/shard_map/bit,bth->bih/dot_general | solution.py:74
  97.6 0.0 reduce-scatter.4.cloned.1.call-update
  97.6 0.0 copy-start.2
  97.6 0.0 copy-start.4
  97.6 6.4 %fusion.16 = f32[2,512,512]{1,2,0:S(1)} fusion(bf16[2,512,2048]{2,1,0:T(8,128)(2,1)} %get-tuple-element.5, bf16[2,2048,512]{2,1,0:T(8,128)(2,1)} %param.11), kind=kOutput, calls=%fused_computation.27 | convolution fusion | flops 2147483648 | bytes 10485760
  104.0 0.3 fusion.9
  104.3 0.0 copy-done.4
  104.4 3.7 %fusion.18 = f32[2,512,512]{2,1,0:T(8,128)} fusion(bf16[2,512,2048]{2,1,0:T(8,128)(2,1)S(1)} %copy-done.4, bf16[2,512,2048]{2,1,0:T(8,128)(2,1)S(1)} %copy-done.2), kind=kOutput, calls=%fused_computation.29 | convolution fusion | flops 2147483648 | bytes 10485760 | tf_op jit(solution)/shard_map/bth,bih->bit/dot_general | solution.py:90
  108.0 7.0 %fusion.8 = bf16[2,512,512]{2,1,0:T(8,128)(2,1)S(1)} fusion(s32[2,512]{1,0:T(2,128)S(1)} %copy-done.3, f32[2,512,512]{2,1,0:T(8,128)} %fusion.18, bf16[2,512,2048]{2,1,0:T(8,128)(2,1)} %get-tuple-element.7, bf16[2,512,2048]{2,1,0:T(8,128)(2,1)} %param.10), kind=kOutput, calls=%fused_computation.19 | convolution fusion | flops 2686976000 | bytes 11538432 | tf_op jit(solution)/shard_map/bij,bit->bjt/dot_general | solution.py:95
  115.0 0.2 pad_maximum_fusion.1
  115.2 0.2 copy.58
  115.5 32.9 %all_to_all.30 = bf16[2,16,2,32,512]{4,3,2,0,1:T(8,128)(2,1)S(1)} all-to-all(bf16[2,16,2,32,512]{4,3,2,0,1:T(8,128)(2,1)S(1)} %copy.58), channel_id=1, replica_groups=mesh['dp'=16,'mp'=8] {'mp'}, dimensions={1} | all-to-all | bytes 4194304 | tf_op jit(solution)/shard_map/all_to_all | solution.py:101
  148.4 0.2 fusion.13
  148.6 1.1 copy.60
  149.7 1.1 copy.59
  150.8 36.0 %reduce-scatter.8.cloned.1.call-done = bf16[2,128,512]{2,1,0:T(8,128)(2,1)} async-done(((bf16[2,2048,512]{2,1,0:T(8,128)(2,1)}), bf16[2,128,512]{2,1,0:T(8,128)(2,1)}) %reduce-scatter.8.cloned.1.call-update) | async-done | bytes 262160 | tf_op jit(solution)/shard_map/reduce_scatter | solution.py:57
  186.7 1.8 convert_element_type.57
  188.5 81.7 %reduce-scatter.6.cloned.1.call-done = bf16[2,32,2048]{2,1,0:T(8,128)(2,1)} async-done(((bf16[2,512,2048]{2,1,0:T(8,128)(2,1)}), bf16[2,32,2048]{2,1,0:T(8,128)(2,1)}) %reduce-scatter.6.cloned.1.call-update) | async-done | bytes 262160 | tf_op jit(solution)/shard_map/reduce_scatter | solution.py:84
  270.2 1.8 convert_element_type.55
  272.0 81.7 %reduce-scatter.4.cloned.1.call-done = bf16[2,32,2048]{2,1,0:T(8,128)(2,1)} async-done(((bf16[2,512,2048]{2,1,0:T(8,128)(2,1)}), bf16[2,32,2048]{2,1,0:T(8,128)(2,1)}) %reduce-scatter.4.cloned.1.call-update) | async-done | bytes 262160 | tf_op jit(solution)/shard_map/reduce_scatter | solution.py:81
  353.6 1.8 convert_element_type.53
  (2 shorter events, 0.0 us)
Async XLA Ops:
  10.5 37.0 %all-to-all-start = ((bf16[2,2,16,32,512]{4,3,1,0,2:T(8,128)(2,1)}), bf16[2,2,16,32,512]{4,3,1,0,2:T(8,128)(2,1)S(1)}, u32[]{:S(2)}, u32[]{:S(2)}) async-start(bf16[2,2,16,32,512]{4,3,1,0,2:T(8,128)(2,1)} %copy.49), calls=%async_computation | async-start | bytes 4194304 | tf_op jit(solution)/shard_map/all_to_all | solution.py:29
  16.2 170.5 %reduce-scatter.8.cloned.1.call-start = ((), (), s32[]{:S(2)}) async-start(), calls=%async_computation.7 | async-start | bytes 4456448 | tf_op jit(solution)/shard_map/reduce_scatter | solution.py:57
  47.9 0.7 copy-start.3
  47.9 2.2 copy-start
  50.1 5.6 %copy-start.1 = (bf16[2,512,2048]{2,1,0:T(8,128)(2,1)S(1)}, bf16[2,512,2048]{2,1,0:T(8,128)(2,1)}, u32[]{:S(2)}) copy-start(bf16[2,512,2048]{2,1,0:T(8,128)(2,1)} %param.9) | copy-start | bytes 12582916
  84.2 186.0 %reduce-scatter.6.cloned.1.call-start = ((), (), s32[]{:S(2)}) async-start(), calls=%async_computation.6 | async-start | bytes 4456448 | tf_op jit(solution)/shard_map/reduce_scatter | solution.py:84
  90.8 262.8 %reduce-scatter.4.cloned.1.call-start = ((), (), s32[]{:S(2)}) async-start(), calls=%async_computation.5 | async-start | bytes 4456448 | tf_op jit(solution)/shard_map/reduce_scatter | solution.py:81
  97.6 6.7 %copy-start.2 = (bf16[2,512,2048]{2,1,0:T(8,128)(2,1)S(1)}, bf16[2,512,2048]{2,1,0:T(8,128)(2,1)}, u32[]{:S(2)}) copy-start(bf16[2,512,2048]{2,1,0:T(8,128)(2,1)} %param.9) | copy-start | bytes 12582916
  97.6 6.7 %copy-start.4 = (bf16[2,512,2048]{2,1,0:T(8,128)(2,1)S(1)}, bf16[2,512,2048]{2,1,0:T(8,128)(2,1)}, u32[]{:S(2)}) copy-start(bf16[2,512,2048]{2,1,0:T(8,128)(2,1)} %get-tuple-element.6) | copy-start | bytes 12582916
Sparse Core Ops, SparseCore 0:
  84.3 102.3 reduce-scatter.7
  190.8 79.3 reduce-scatter.5
  274.3 79.3 reduce-scatter.3

commit v2 on v1

--- a/solution.py
+++ b/solution.py
@@ -1,6 +1,7 @@
 import jax
 import jax.numpy as jnp
 from jax import lax
+from jax.sharding import Mesh
 from jax.sharding import PartitionSpec as P
 
 input_scale = 2.0
@@ -13,13 +14,27 @@
     return (block_perm[:, :, None] == targets).astype(jnp.bfloat16)
 
 
+def reduce_rows(part):
+    blocks, rows, cols = part.shape
+    n_chip = lax.axis_size("dpc")
+    core = lax.axis_index("core")
+    view = part.reshape(blocks, n_chip, 2, rows // (2 * n_chip), cols)
+    mine = jnp.where(core == 0, view[:, :, 0], view[:, :, 1])
+    other = jnp.where(core == 0, view[:, :, 1], view[:, :, 0])
+    got = lax.ppermute(other, "core", perm=[(0, 1), (1, 0)])
+    summed = (mine.astype(jnp.float32) + got.astype(jnp.float32)).astype(jnp.bfloat16)
+    summed = summed.reshape(blocks, rows // 2, cols)
+    return lax.psum_scatter(summed, "dpc", scatter_dimension=1, tiled=True).astype(jnp.float32)
+
+
 def local(features, cotangent, block_perm, w_gate, w_up, w_down):
     tok_count = features.shape[1]
     blocks_here = w_gate.shape[0]
     inner = w_gate.shape[1]
     hidden_width = w_gate.shape[2]
     n_mp = lax.axis_size("mp")
-    n_dp = lax.axis_size("dp")
+    n_chip = lax.axis_size("dpc")
+    n_dp = n_chip * lax.axis_size("core")
     block_total = blocks_here * n_mp
     piece = inner // block_total
     s_here = features.shape[0] // (block_total * piece)
@@ -49,14 +64,11 @@
     hidden = (act * up).astype(jnp.bfloat16)
     down_view = w_down.reshape(blocks_here, hidden_width, block_total, piece)
 
-    chunk = n_dp
     down_part = (
         jnp.einsum("bth,sbkt->bhsk", hidden, cot_blocks, preferred_element_type=jnp.float32)
         * (output_scale * grad_scale)
     ).astype(jnp.bfloat16)
-    down_grad = lax.psum_scatter(
-        down_part.reshape(blocks_here, hidden_width, inner), "dp", scatter_dimension=1, tiled=True
-    ).astype(jnp.float32)
+    down_grad = reduce_rows(down_part.reshape(blocks_here, hidden_width, inner))
 
     mixed = (
         jnp.einsum("bth,bhsk->sbkt", hidden, down_view, preferred_element_type=jnp.float32)
@@ -78,12 +90,8 @@
         jnp.einsum("bit,bth->bih", feat_p, d_up, preferred_element_type=jnp.float32)
         * (input_scale * grad_scale)
     ).astype(jnp.bfloat16)
-    gate_grad = lax.psum_scatter(gate_part, "dp", scatter_dimension=1, tiled=True).astype(
-        jnp.float32
-    )
-    up_grad = lax.psum_scatter(up_part, "dp", scatter_dimension=1, tiled=True).astype(
-        jnp.float32
-    )
+    gate_grad = reduce_rows(gate_part)
+    up_grad = reduce_rows(up_part)
 
     d_mixed_p = (
         (
@@ -101,14 +109,17 @@
     back = lax.all_to_all(back, "mp", split_axis=1, concat_axis=2, tiled=True)
     outputs = back[0].reshape(features.shape)
     d_features = back[1].reshape(features.shape)
-    del chunk
     return (outputs, d_features, gate_grad, up_grad, down_grad)
 
 
 def solution(mesh):
+    dp_size = mesh.shape["dp"]
+    devices = mesh.devices.reshape(dp_size // 2, 2, mesh.shape["mp"])
+    mesh = Mesh(devices, ("dpc", "core", "mp"))
+    dp = ("dpc", "core")
     placed = (
-        P("mp", "dp"),
-        P("mp", "dp"),
+        P("mp", dp),
+        P("mp", dp),
         P("mp", None),
         P("mp", None, None),
         P("mp", None, None),
@@ -119,11 +130,11 @@
         mesh=mesh,
         in_specs=placed,
         out_specs=(
-            P("mp", "dp"),
-            P("mp", "dp"),
-            P("mp", "dp", None),
-            P("mp", "dp", None),
-            P("mp", "dp", None),
+            P("mp", dp),
+            P("mp", dp),
+            P("mp", dp, None),
+            P("mp", dp, None),
+            P("mp", dp, None),
         ),
         check_vma=False,
     )

time: 363 us -> 382 us (1.052)
  local copies, waits for them, and re-layouts: 18.6 us -> 49.7 us
  waiting for transfers between devices: 224 us -> 209 us
  other arithmetic: 7.57 us -> 17.6 us
  matrix products: 58.9 us -> 54.6 us
    reduce_scatter x3, waiting for transfers between devices: 199 us -> 171 us  [reduce_rows(): lax.psum_scatter(summed, 'dpc', scatter_dimension=1, tiled=True)]
    unnamed x11 -> x15, local copies, waits for them, and re-layouts: 7.46 us -> 26.9 us
    ppermute x0 -> x3, waiting for transfers between devices: none -> 12.2 us  [reduce_rows(): got = lax.ppermute(other, 'core', perm=[(0, 1), (1, 0)])]
    slice x0 -> x1, local copies, waits for them, and re-layouts: none -> 10.1 us  [reduce_rows(): mine = jnp.where(core == 0, view[:, :, 0], view[:, :, 1])]
    another operation x0 -> x1, local copies, waits for them, and re-layouts: none -> 7.68 us  [reduce_rows(): view = part.reshape(blocks, n_chip, 2, rows // (2 * n_chip), cols)]
    convert_element_type x3 -> x6, other arithmetic: 5.35 us -> 13 us  [the longest x3 7.65 us: reduce_rows(): (mine.astype(jnp.float32) + got.astype(jnp.float32)).astype(jnp.bfloat16)]
    reshape x1 -> x0, local copies, waits for them, and re-layouts: 6.19 us -> none  [local(): down_part.reshape(blocks_here, hidden_width, inner)]
  transfers between devices with their start and end apart: 4 -> 7, of which waited for: 4 -> 7; matrix products, arithmetic and copies ran while one was open for 12% -> 12% of each run, Pallas kernels for 0% -> 0%
where the time goes in v2:
time: 382 us; the launch traced here: 380 us
  waiting for transfers between devices  209 us (55%)
  matrix products  54.6 us (14%)
  local copies, waits for them, and re-layouts  49.7 us (13%)
  blocking collectives  29.4 us (8%)
  other arithmetic  17.6 us (5%)
  between operations  14 us (4%)
  starting transfers between devices  6.62 us (2%)
    reduce_scatter x3, waiting for transfers between devices, reduce_rows(): lax.psum_scatter(summed, 'dpc', scatter_dimension=1, tiled=True)  171 us
    all_to_all x1, blocking collectives, local(): back = lax.all_to_all(back, 'mp', split_axis=1, concat_axis=2, tiled=True)  29.4 us
    unnamed x15, local copies, waits for them, and re-layouts  26.9 us
    all_to_all x1, waiting for transfers between devices, local(): both = lax.all_to_all(both, 'mp', split_axis=2, concat_axis=1, tiled=True)  24.9 us
    dot_general x1, matrix products, local(): jnp.einsum('bit,bih->bth', feat_p, w_up, preferred_element_type=jnp.float32)  13.3 us
    ppermute x3, waiting for transfers between devices, reduce_rows(): got = lax.ppermute(other, 'core', perm=[(0, 1), (1, 0)])  12.2 us
    slice x1, local copies, waits for them, and re-layouts, reduce_rows(): mine = jnp.where(core == 0, view[:, :, 0], view[:, :, 1])  10.1 us
    another operation x1, local copies, waits for them, and re-layouts, reduce_rows(): view = part.reshape(blocks, n_chip, 2, rows // (2 * n_chip), cols)  7.68 us
  transfers between devices with their start and end apart: 7, of which 7 were waited for; matrix products, arithmetic and copies ran while one was open for 12% of the time, Pallas kernels for 0%

profile of v2, /device:TPU:0, one launch (start us, length us, event | category | flops | bytes accessed | tf_op | source)
XLA Modules:
  0.0 380.4 jit_solution(9643830582617685784)
XLA Ops:
  7.2 1.7 pad_maximum_fusion
  8.9 1.6 copy.80
  10.5 5.8 %all-to-all-start = ((bf16[2,2,16,32,512]{4,3,1,0,2:T(8,128)(2,1)}), bf16[2,2,16,32,512]{4,3,1,0,2:T(8,128)(2,1)S(1)}, u32[]{:S(2)}, u32[]{:S(2)}) async-start(bf16[2,2,16,32,512]{4,3,1,0,2:T(8,128)(2,1)} %copy.80), calls=%async_computation | async-start | bytes 4194304 | tf_op jit(solution)/shard_map/all_to_all | solution.py:44
  16.3 6.3 %copy.87 = bf16[2,2048,512]{1,2,0:T(8,128)(2,1)} copy(bf16[2,2048,512]{2,1,0:T(8,128)(2,1)} %param.11) | data formatting | bytes 8388608 | tf_op args[5]
  22.6 24.9 %all-to-all-done = bf16[2,2,16,32,512]{4,3,1,0,2:T(8,128)(2,1)S(1)} async-done(((bf16[2,2,16,32,512]{4,3,1,0,2:T(8,128)(2,1)}), bf16[2,2,16,32,512]{4,3,1,0,2:T(8,128)(2,1)S(1)}, u32[]{:S(2)}, u32[]{:S(2)}) %all-to-all-start) | async-done | bytes 2097184 | tf_op jit(solution)/shard_map/all_to_all | solution.py:44
  47.5 0.2 copy.81
  47.7 0.2 fusion.20
  48.0 0.1 copy.82
  48.3 0.4 copy-done.4
  48.6 0.8 fusion.12
  49.4 0.8 copy-done.2
  50.1 2.4 fusion.21
  52.5 5.6 %fusion.23 = f32[2,512,2048,1]{2,1,3,0:T(8,128)} fusion(bf16[16,2,32,512]{3,2,0,1:T(8,128)(2,1)S(1)} %bitcast.126, bf16[2,2048,16,32]{1,3,2,0:T(8,128)(2,1)S(1)} %bitcast.121), kind=kOutput, calls=%fused_computation.43 | convolution fusion | flops 2147483648 | bytes 13631488 | tf_op jit(solution)/shard_map/sbkt,bhsk->bth/dot_general | solution.py:79
  58.2 13.3 %multiply_convert_fusion.5 = (bf16[2,512,2048]{2,1,0:T(8,128)(2,1)}, bf16[2,512,2048]{2,1,0:T(8,128)(2,1)}, bf16[2,512,2048]{2,1,0:T(8,128)(2,1)}) fusion(f32[2,512,2048]{2,1,0:T(8,128)S(1)} %fusion.21, f32[2,512,2048,1]{2,1,3,0:T(8,128)} %fusion.23, bf16[2,512,512]{2,1,0:T(8,128)(2,1)S(1)} %fusion.12, bf16[2,512,2048]{2,1,0:T(8,128)(2,1)} %param.10), kind=kOutput, calls=%fused_computation.6 | convolution fusion | flops 2185232384 | bytes 34603008 | tf_op jit(solution)/shard_map/bit,bih->bth/dot_general | solution.py:59
  71.5 6.5 %multiply_convert_fusion = bf16[2,2048,16,32]{1,3,2,0:T(8,128)(2,1)} fusion(bf16[16,2,32,512]{3,2,0,1:T(8,128)(2,1)S(1)} %bitcast.127, bf16[2,512,2048]{2,1,0:T(8,128)(2,1)} %get-tuple-element.5), kind=kOutput, calls=%fused_computation.1 | convolution fusion | flops 2151677952 | bytes 9437184 | tf_op jit(solution)/shard_map/bth,sbkt->bhsk/dot_general | solution.py:68
  78.0 7.7 %reshape_reshape.3 = bf16[2,8,2,128,512]{3,2,1,4,0:T(2,128)(2,1)} reshape(bf16[2,2048,16,32]{1,3,2,0:T(8,128)(2,1)} %multiply_convert_fusion) | data formatting | bytes 8388608 | tf_op jit(solution)/shard_map/reshape;reshape | solution.py:21
  85.7 10.1 %fusion.18 = (bf16[2,8,1,128,512]{3,2,1,4,0:T(2,128)(2,1)}, bf16[2,8,1,128,512]{3,2,1,4,0:T(2,128)(2,1)}) fusion(bf16[2,8,2,128,512]{3,2,1,4,0:T(2,128)(2,1)} %reshape_reshape.3), kind=kLoop, calls=%fused_computation.38 | loop fusion | bytes 8388608 | tf_op jit(solution)/shard_map/slice | solution.py:22
  95.8 9.0 %copy.108 = bf16[2,8,1,128,512]{4,3,1,0,2:T(8,128)(2,1)S(1)} copy(bf16[2,8,1,128,512]{3,2,1,4,0:T(2,128)(2,1)} %get-tuple-element.8) | data formatting | bytes 4194304
  104.8 10.5 %copy.109 = bf16[2,8,1,128,512]{4,3,1,0,2:T(8,128)(2,1)} copy(bf16[2,8,1,128,512]{3,2,1,4,0:T(2,128)(2,1)} %get-tuple-element.9) | data formatting | bytes 4194304
  115.3 2.0 select_bitcast_fusion
  117.3 4.1 %collective-permute-done.2 = bf16[2,8,128,512]{3,2,1,0:T(8,128)(2,1)S(1)} collective-permute-done((bf16[2,8,128,512]{3,2,1,0:T(8,128)(2,1)S(1)}, bf16[2,8,128,512]{3,2,1,0:T(8,128)(2,1)S(1)}, u32[]{:S(2)}, u32[]{:S(2)}) %collective-permute-start.2) | collective-permute-done | bytes 2097184 | tf_op jit(solution)/shard_map/ppermute | solution.py:24
  121.5 2.3 fusion.1
  123.9 4.5 %multiply_convert_fusion.1 = bf16[2,512,2048]{2,1,0:T(8,128)(2,1)S(1)} fusion(bf16[2,512,512]{2,1,0:T(8,128)(2,1)S(1)} %fusion.12, bf16[2,512,2048]{2,1,0:T(8,128)(2,1)} %get-tuple-element.7), kind=kOutput, calls=%fused_computation.2 | convolution fusion | flops 2151677952 | bytes 9437184 | tf_op jit(solution)/shard_map/bit,bth->bih/dot_general | solution.py:90
  128.4 0.2 select_bitcast_fusion.1
  128.7 0.2 collective-permute-start.1
  128.9 4.0 %collective-permute-done.1 = bf16[2,8,32,2048]{3,2,1,0:T(8,128)(2,1)S(1)} collective-permute-done((bf16[2,8,32,2048]{3,2,1,0:T(8,128)(2,1)S(1)}, bf16[2,8,32,2048]{3,2,1,0:T(8,128)(2,1)S(1)}, u32[]{:S(2)}, u32[]{:S(2)}) %collective-permute-start.1) | collective-permute-done | bytes 2097184 | tf_op jit(solution)/shard_map/ppermute | solution.py:24
  132.9 2.7 fusion.4
  135.6 4.5 %multiply_convert_fusion.2 = bf16[2,512,2048]{2,1,0:T(8,128)(2,1)S(1)} fusion(bf16[2,512,512]{2,1,0:T(8,128)(2,1)S(1)} %fusion.12, bf16[2,512,2048]{2,1,0:T(8,128)(2,1)} %get-tuple-element.6), kind=kOutput, calls=%fused_computation.3 | convolution fusion | flops 2151677952 | bytes 9437184 | tf_op jit(solution)/shard_map/bit,bth->bih/dot_general | solution.py:86
  140.2 0.2 fusion.8
  140.4 0.4 collective-permute-start
  140.9 4.0 %collective-permute-done = bf16[2,8,32,2048]{3,2,1,0:T(8,128)(2,1)S(1)} collective-permute-done((bf16[2,8,32,2048]{3,2,1,0:T(8,128)(2,1)S(1)}, bf16[2,8,32,2048]{3,2,1,0:T(8,128)(2,1)S(1)}, u32[]{:S(2)}, u32[]{:S(2)}) %collective-permute-start) | collective-permute-done | bytes 2097184 | tf_op jit(solution)/shard_map/ppermute | solution.py:24
  144.9 2.7 fusion.5
  147.6 6.1 %fusion.22 = f32[2,512,512]{1,2,0:S(1)} fusion(bf16[2,512,2048]{2,1,0:T(8,128)(2,1)} %get-tuple-element.5, bf16[2,2048,512]{2,1,0:T(8,128)(2,1)} %param.11), kind=kOutput, calls=%fused_computation.42 | convolution fusion | flops 2147483648 | bytes 10485760
  153.7 0.3 fusion.14
  154.0 3.7 fusion.24
  157.7 7.1 %fusion.13 = bf16[2,512,512]{2,1,0:T(8,128)(2,1)S(1)} fusion(s32[2,512]{1,0:T(2,128)S(1)} %copy-done.4, f32[2,512,512]{2,1,0:T(8,128)} %fusion.24, bf16[2,512,2048]{2,1,0:T(8,128)(2,1)} %get-tuple-element.7, bf16[2,512,2048]{2,1,0:T(8,128)(2,1)} %param.10), kind=kOutput, calls=%fused_computation.33 | convolution fusion | flops 2686976000 | bytes 11538432 | tf_op jit(solution)/shard_map/bij,bit->bjt/dot_general | solution.py:103
  164.8 0.2 pad_maximum_fusion.1
  165.0 0.2 copy.89
  165.2 29.4 %all_to_all.30 = bf16[2,16,2,32,512]{4,3,2,0,1:T(8,128)(2,1)S(1)} all-to-all(bf16[2,16,2,32,512]{4,3,2,0,1:T(8,128)(2,1)S(1)} %copy.89), channel_id=1, replica_groups=mesh['dpc'=8,'core'=2,'mp'=8] {'mp'}, dimensions={1} | all-to-all | bytes 4194304 | tf_op jit(solution)/shard_map/all_to_all | solution.py:109
  194.7 0.2 fusion.19
  194.9 1.1 copy.90
  196.0 1.1 copy.91
  197.1 16.6 %reduce-scatter.8.cloned.1.call-done = bf16[2,128,512]{2,1,0:T(8,128)(2,1)} async-done(((bf16[2,1024,512]{2,1,0:T(8,128)(2,1)}), bf16[2,128,512]{2,1,0:T(8,128)(2,1)}) %reduce-scatter.8.cloned.1.call-update) | async-done | bytes 262160 | tf_op jit(solution)/shard_map/reduce_scatter | solution.py:27
  213.7 1.8 convert_element_type.105
  215.5 77.4 %reduce-scatter.6.cloned.1.call-done = bf16[2,32,2048]{2,1,0:T(8,128)(2,1)} async-done(((bf16[2,256,2048]{2,1,0:T(8,128)(2,1)}), bf16[2,32,2048]{2,1,0:T(8,128)(2,1)}) %reduce-scatter.6.cloned.1.call-update) | async-done | bytes 262160 | tf_op jit(solution)/shard_map/reduce_scatter | solution.py:27
  292.9 1.8 convert_element_type.99
  294.7 77.4 %reduce-scatter.4.cloned.1.call-done = bf16[2,32,2048]{2,1,0:T(8,128)(2,1)} async-done(((bf16[2,256,2048]{2,1,0:T(8,128)(2,1)}), bf16[2,32,2048]{2,1,0:T(8,128)(2,1)}) %reduce-scatter.4.cloned.1.call-update) | async-done | bytes 262160 | tf_op jit(solution)/shard_map/reduce_scatter | solution.py:27
  372.1 1.8 convert_element_type.93
  (19 shorter events, 0.5 us)
Async XLA Ops:
  10.5 37.0 %all-to-all-start = ((bf16[2,2,16,32,512]{4,3,1,0,2:T(8,128)(2,1)}), bf16[2,2,16,32,512]{4,3,1,0,2:T(8,128)(2,1)S(1)}, u32[]{:S(2)}, u32[]{:S(2)}) async-start(bf16[2,2,16,32,512]{4,3,1,0,2:T(8,128)(2,1)} %copy.80), calls=%async_computation | async-start | bytes 4194304 | tf_op jit(solution)/shard_map/all_to_all | solution.py:44
  16.3 197.5 %reduce-scatter.8.cloned.1.call-start = ((), (), s32[]{:S(2)}) async-start(), calls=%async_computation.7 | async-start | bytes 2359296 | tf_op jit(solution)/shard_map/reduce_scatter | solution.py:27
  47.9 0.7 copy-start.4
  47.9 2.2 copy-start.2
  50.1 2.4 copy-start.1
  115.3 6.2 %copy-start = (bf16[2,8,1,128,512]{4,3,1,0,2:T(8,128)(2,1)S(1)}, bf16[2,8,1,128,512]{4,3,1,0,2:T(8,128)(2,1)}, u32[]{:S(2)}) copy-start(bf16[2,8,1,128,512]{4,3,1,0,2:T(8,128)(2,1)} %copy.109) | copy-start | bytes 6291460
  117.2 4.2 %collective-permute-start.2 = (bf16[2,8,128,512]{3,2,1,0:T(8,128)(2,1)S(1)}, bf16[2,8,128,512]{3,2,1,0:T(8,128)(2,1)S(1)}, u32[]{:S(2)}, u32[]{:S(2)}) collective-permute-start(bf16[2,8,128,512]{3,2,1,0:T(8,128)(2,1)S(1)} %select_bitcast_fusion), channel_id=1, source_target_pairs={{0,8},{8,0},{1,9},{9,1},{2,10},{10,2},{3,11},{11,3},{4,12},{12,4},... | collective-permute-start | bytes 6291464 | tf_op jit(solution)/shard_map/ppermute | solution.py:24
  123.8 169.1 %reduce-scatter.6.cloned.1.call-start = ((), (), s32[]{:S(2)}) async-start(), calls=%async_computation.6 | async-start | bytes 2359296 | tf_op jit(solution)/shard_map/reduce_scatter | solution.py:27
  128.7 4.2 %collective-permute-start.1 = (bf16[2,8,32,2048]{3,2,1,0:T(8,128)(2,1)S(1)}, bf16[2,8,32,2048]{3,2,1,0:T(8,128)(2,1)S(1)}, u32[]{:S(2)}, u32[]{:S(2)}) collective-permute-start(bf16[2,8,32,2048]{3,2,1,0:T(8,128)(2,1)S(1)} %select_bitcast_fusion.1), channel_id=1, source_target_pairs={{0,8},{8,0},{1,9},{9,1},{2,10},{10,2},{3,11},{11,3},{4,12},{12,4},... | collective-permute-start | bytes 6291464 | tf_op jit(solution)/shard_map/ppermute | solution.py:24
  135.6 236.5 %reduce-scatter.4.cloned.1.call-start = ((), (), s32[]{:S(2)}) async-start(), calls=%async_computation.5 | async-start | bytes 2359296 | tf_op jit(solution)/shard_map/reduce_scatter | solution.py:27
  140.4 4.5 %collective-permute-start = (bf16[2,8,32,2048]{3,2,1,0:T(8,128)(2,1)S(1)}, bf16[2,8,32,2048]{3,2,1,0:T(8,128)(2,1)S(1)}, u32[]{:S(2)}, u32[]{:S(2)}) collective-permute-start(bf16[2,8,32,2048]{3,2,1,0:T(8,128)(2,1)S(1)} %fusion.8), channel_id=1, source_target_pairs={{0,8},{8,0},{1,9},{9,1},{2,10},{10,2},{3,11},{11,3},{4,12},{12,4},... | collective-permute-start | bytes 6291464 | tf_op jit(solution)/shard_map/ppermute | solution.py:24
  147.6 6.4 %copy-start.3 = (bf16[2,512,2048]{2,1,0:T(8,128)(2,1)S(1)}, bf16[2,512,2048]{2,1,0:T(8,128)(2,1)}, u32[]{:S(2)}) copy-start(bf16[2,512,2048]{2,1,0:T(8,128)(2,1)} %param.9) | copy-start | bytes 12582916
  147.6 6.4 %copy-start.5 = (bf16[2,512,2048]{2,1,0:T(8,128)(2,1)S(1)}, bf16[2,512,2048]{2,1,0:T(8,128)(2,1)}, u32[]{:S(2)}) copy-start(bf16[2,512,2048]{2,1,0:T(8,128)(2,1)} %get-tuple-element.6) | copy-start | bytes 12582916
Sparse Core Ops, SparseCore 0:
  124.0 89.7 reduce-scatter.7
  217.5 75.3 reduce-scatter.5
  296.7 75.3 reduce-scatter.3

commit v3 on v2

--- a/solution.py
+++ b/solution.py
@@ -14,17 +14,26 @@
     return (block_perm[:, :, None] == targets).astype(jnp.bfloat16)
 
 
-def reduce_rows(part):
-    blocks, rows, cols = part.shape
-    n_chip = lax.axis_size("dpc")
-    core = lax.axis_index("core")
-    view = part.reshape(blocks, n_chip, 2, rows // (2 * n_chip), cols)
-    mine = jnp.where(core == 0, view[:, :, 0], view[:, :, 1])
-    other = jnp.where(core == 0, view[:, :, 1], view[:, :, 0])
-    got = lax.ppermute(other, "core", perm=[(0, 1), (1, 0)])
-    summed = (mine.astype(jnp.float32) + got.astype(jnp.float32)).astype(jnp.bfloat16)
-    summed = summed.reshape(blocks, rows // 2, cols)
-    return lax.psum_scatter(summed, "dpc", scatter_dimension=1, tiled=True).astype(jnp.float32)
+def tree_reduce(part):
+    lead, rows, cols = part.shape
+    n_dy = lax.axis_size("dy")
+    tail = rows // (n_dy * 4)
+    acc = part.reshape(lead, n_dy // 2, 2, 2, 2, tail, cols)
+    dy = lax.axis_index("dy")
+    steps = (
+        ("core", 4, [(0, 1), (1, 0)], lax.axis_index("core")),
+        ("dy", 2, [(i, i ^ 1) for i in range(n_dy)], dy % 2),
+        ("dz", 3, [(0, 1), (1, 0)], lax.axis_index("dz")),
+        ("dy", 1, [(i, i ^ 2) for i in range(n_dy)], dy // 2),
+    )
+    total = None
+    for name, dim, pairs, bit in steps:
+        mine = lax.dynamic_index_in_dim(acc, bit, dim, keepdims=True)
+        other = lax.dynamic_index_in_dim(acc, 1 - bit, dim, keepdims=True)
+        got = lax.ppermute(other, name, perm=pairs)
+        total = mine.astype(jnp.float32) + got.astype(jnp.float32)
+        acc = total.astype(jnp.bfloat16)
+    return total.reshape(lead, tail, cols)
 
 
 def local(features, cotangent, block_perm, w_gate, w_up, w_down):
@@ -33,8 +42,7 @@
     inner = w_gate.shape[1]
     hidden_width = w_gate.shape[2]
     n_mp = lax.axis_size("mp")
-    n_chip = lax.axis_size("dpc")
-    n_dp = n_chip * lax.axis_size("core")
+    n_dp = lax.axis_size("dy") * lax.axis_size("dz") * lax.axis_size("core")
     block_total = blocks_here * n_mp
     piece = inner // block_total
     s_here = features.shape[0] // (block_total * piece)
@@ -68,7 +76,7 @@
         jnp.einsum("bth,sbkt->bhsk", hidden, cot_blocks, preferred_element_type=jnp.float32)
         * (output_scale * grad_scale)
     ).astype(jnp.bfloat16)
-    down_grad = reduce_rows(down_part.reshape(blocks_here, hidden_width, inner))
+    down_grad = tree_reduce(down_part.reshape(blocks_here, hidden_width, inner))
 
     mixed = (
         jnp.einsum("bth,bhsk->sbkt", hidden, down_view, preferred_element_type=jnp.float32)
@@ -90,8 +98,11 @@
         jnp.einsum("bit,bth->bih", feat_p, d_up, preferred_element_type=jnp.float32)
         * (input_scale * grad_scale)
     ).astype(jnp.bfloat16)
-    gate_grad = reduce_rows(gate_part)
-    up_grad = reduce_rows(up_part)
+    gate_up = tree_reduce(
+        jnp.concatenate([gate_part, up_part]).reshape(2 * blocks_here, inner, hidden_width)
+    )
+    gate_grad = gate_up[:blocks_here]
+    up_grad = gate_up[blocks_here:]
 
     d_mixed_p = (
         (
@@ -114,9 +125,9 @@
 
 def solution(mesh):
     dp_size = mesh.shape["dp"]
-    devices = mesh.devices.reshape(dp_size // 2, 2, mesh.shape["mp"])
-    mesh = Mesh(devices, ("dpc", "core", "mp"))
-    dp = ("dpc", "core")
+    devices = mesh.devices.reshape(dp_size // 4, 2, 2, mesh.shape["mp"])
+    mesh = Mesh(devices, ("dy", "dz", "core", "mp"))
+    dp = ("dy", "dz", "core")
     placed = (
         P("mp", dp),
         P("mp", dp),

time: 382 us -> 262 us (0.69)
  waiting for transfers between devices: 209 us -> 80.1 us
  blocking collectives: 29.4 us -> 0 us
  local copies, waits for them, and re-layouts: 49.7 us -> 69.1 us
  starting transfers between devices: 6.62 us -> 25.3 us
  between operations: 14 us -> 0.91 us
  other arithmetic: 17.6 us -> 25.6 us
  matrix products: 54.6 us -> 58.8 us
    reduce_scatter x3 -> x0, waiting for transfers between devices: 171 us -> none  [reduce_rows(): lax.psum_scatter(summed, 'dpc', scatter_dimension=1, tiled=True)]
    ppermute x3 -> x8, waiting for transfers between devices: 12.2 us -> 55.1 us  [tree_reduce(): got = lax.ppermute(other, name, perm=pairs)]
    all_to_all x1 -> x0, blocking collectives: 29.4 us -> none  [local(): back = lax.all_to_all(back, 'mp', split_axis=1, concat_axis=2, tiled=True)]
    dynamic_slice x0 -> x8, local copies, waits for them, and re-layouts: none -> 21.7 us  [the longest x2 18.2 us: tree_reduce(): mine = lax.dynamic_index_in_dim(acc, bit, dim, keepdims=True)]
    ppermute x3 -> x8, starting transfers between devices: 0.74 us -> 15 us  [tree_reduce(): got = lax.ppermute(other, name, perm=pairs)]
    slice x1, local copies, waits for them, and re-layouts: 10.1 us -> 1.07 us  [local(): up_grad = gate_up[blocks_here:]]
    concatenate x0 -> x1, other arithmetic: none -> 7.46 us  [local(): jnp.concatenate([gate_part, up_part])]
    all_to_all x0 -> x1, starting transfers between devices: none -> 4.61 us  [local(): back = lax.all_to_all(back, 'mp', split_axis=1, concat_axis=2, tiled=True)]
  transfers between devices with their start and end apart: 7 -> 10, of which waited for: 7 -> 6; matrix products, arithmetic and copies ran while one was open for 12% -> 37% of each run, Pallas kernels for 0% -> 0%
where the time goes in v3:
time: 262 us; the launch traced here: 260 us
  waiting for transfers between devices  80.1 us (31%)
  local copies, waits for them, and re-layouts  69.1 us (26%)
  matrix products  58.8 us (22%)
  other arithmetic  25.6 us (10%)
  starting transfers between devices  25.3 us (10%)
    ppermute x8, waiting for transfers between devices, tree_reduce(): got = lax.ppermute(other, name, perm=pairs)  55.1 us
    unnamed x32, local copies, waits for them, and re-layouts  30.6 us
    all_to_all x1, waiting for transfers between devices, local(): both = lax.all_to_all(both, 'mp', split_axis=2, concat_axis=1, tiled=True)  25 us
    dynamic_slice x2, local copies, waits for them, and re-layouts, tree_reduce(): mine = lax.dynamic_index_in_dim(acc, bit, dim, keepdims=True)  18.2 us
    ppermute x8, starting transfers between devices, tree_reduce(): got = lax.ppermute(other, name, perm=pairs)  15 us
    convert_element_type x6, other arithmetic, tree_reduce(): acc = total.astype(jnp.bfloat16)  13.9 us
    dot_general x1, matrix products, local(): jnp.einsum('bit,bih->bth', feat_p, w_up, preferred_element_type=jnp.float32)  13.4 us
    dot_general x1, matrix products, local(): jnp.einsum('bij,bit->bjt', onehot, d_mixed_p, preferred_element_type=jnp....  7.95 us
  transfers between devices with their start and end apart: 10, of which 6 were waited for; matrix products, arithmetic and copies ran while one was open for 37% of the time, Pallas kernels for 0%

profile of v3, /device:TPU:0, one launch (start us, length us, event | category | flops | bytes accessed | tf_op | source)
XLA Modules:
  0.0 259.9 jit_solution(17476548397810197380)
XLA Ops:
  0.6 1.7 pad_maximum_fusion.1
  2.4 1.6 copy.61
  4.0 5.8 %all-to-all-start = ((bf16[2,2,16,32,512]{4,3,1,0,2:T(8,128)(2,1)}), bf16[2,2,16,32,512]{4,3,1,0,2:T(8,128)(2,1)S(1)}, u32[]{:S(2)}, u32[]{:S(2)}) async-start(bf16[2,2,16,32,512]{4,3,1,0,2:T(8,128)(2,1)} %copy.61), calls=%async_computation | async-start | bytes 4194304 | tf_op jit(solution)/shard_map/all_to_all | solution.py:52
  9.8 6.3 %copy.68 = bf16[2,2048,512]{1,2,0:T(8,128)(2,1)} copy(bf16[2,2048,512]{2,1,0:T(8,128)(2,1)} %param.11) | data formatting | bytes 8388608 | tf_op args[5]
  16.0 25.0 %all-to-all-done = bf16[2,2,16,32,512]{4,3,1,0,2:T(8,128)(2,1)S(1)} async-done(((bf16[2,2,16,32,512]{4,3,1,0,2:T(8,128)(2,1)}), bf16[2,2,16,32,512]{4,3,1,0,2:T(8,128)(2,1)S(1)}, u32[]{:S(2)}, u32[]{:S(2)}) %all-to-all-start) | async-done | bytes 2097184 | tf_op jit(solution)/shard_map/all_to_all | solution.py:52
  42.1 0.8 fusion.7
  43.6 2.4 fusion.15
  46.0 5.7 %fusion.17 = f32[2,512,2048,1]{2,1,3,0:T(8,128)} fusion(bf16[16,2,32,512]{3,2,0,1:T(8,128)(2,1)S(1)} %bitcast.76, bf16[2,2048,16,32]{1,3,2,0:T(8,128)(2,1)S(1)} %bitcast.73), kind=kOutput, calls=%fused_computation.49 | convolution fusion | flops 2147483648 | bytes 13631488 | tf_op jit(solution)/shard_map/sbkt,bhsk->bth/dot_general | solution.py:87
  51.7 13.4 %multiply_convert_fusion.5 = (bf16[2,512,2048]{2,1,0:T(8,128)(2,1)}, bf16[2,512,2048]{2,1,0:T(8,128)(2,1)}, bf16[2,512,2048]{2,1,0:T(8,128)(2,1)}) fusion(f32[2,512,2048]{2,1,0:T(8,128)S(1)} %fusion.15, f32[2,512,2048,1]{2,1,3,0:T(8,128)} %fusion.17, bf16[2,512,512]{2,1,0:T(8,128)(2,1)S(1)} %fusion.7, bf16[2,512,2048]{2,1,0:T(8,128)(2,1)} %param.10), kind=kOutput, calls=%fused_computation.8 | convolution fusion | flops 2185232384 | bytes 34603008 | tf_op jit(solution)/shard_map/bit,bih->bth/dot_general | solution.py:67
  65.1 6.7 %multiply_convert_fusion.1 = bf16[2,512,2048]{2,1,0:T(8,128)(2,1)} fusion(bf16[2,512,512]{2,1,0:T(8,128)(2,1)S(1)} %fusion.7, bf16[2,512,2048]{2,1,0:T(8,128)(2,1)} %get-tuple-element.7), kind=kOutput, calls=%fused_computation.4 | convolution fusion | flops 2151677952 | bytes 9437184 | tf_op jit(solution)/shard_map/bit,bth->bih/dot_general | solution.py:98
  71.8 4.4 %multiply_convert_fusion.2 = bf16[2,512,2048]{2,1,0:T(8,128)(2,1)} fusion(bf16[2,512,512]{2,1,0:T(8,128)(2,1)S(1)} %fusion.7, bf16[2,512,2048]{2,1,0:T(8,128)(2,1)S(1)} %copy-done.12), kind=kOutput, calls=%fused_computation.5 | convolution fusion | flops 2151677952 | bytes 9437184 | tf_op jit(solution)/shard_map/bit,bth->bih/dot_general | solution.py:94
  76.2 7.5 %pad_maximum_fusion = bf16[4,512,2048]{2,1,0:T(8,128)(2,1)} fusion(bf16[2,512,2048]{2,1,0:T(8,128)(2,1)} %multiply_convert_fusion.1, bf16[2,512,2048]{2,1,0:T(8,128)(2,1)} %multiply_convert_fusion.2), kind=kLoop, calls=%fused_computation | loop fusion | flops 4194304 | bytes 16777216 | tf_op jit(solution)/shard_map/concatenate | solution.py:102
  83.7 6.7 %constant_dynamic-slice_fusion.9 = (bf16[4,2,2,2,1,32,2048]{6,5,4,3,2,1,0:T(8,128)(2,1)}, bf16[4,2,2,2,1,32,2048]{6,5,4,3,2,1,0:T(8,128)(2,1)S(1)}) fusion(bf16[4,2,2,2,2,32,2048]{6,5,4,3,2,1,0:T(8,128)(2,1)} %bitcast.71, s32[]{:T(128)S(6)} %select_n.54, s32[]{:T(128)S(6)} %select_n.55), kind=kLoop, calls=%fused_computation.43 | loop fusion | bytes 16777224 | tf_op jit(solution)/shard_map/jit(dynamic_index_in_dim)/dynamic_slice | solution.py:31
  90.4 2.3 copy.83
  92.7 6.6 %multiply_convert_fusion = bf16[2,2048,16,32]{1,3,2,0:T(8,128)(2,1)} fusion(bf16[16,2,32,512]{3,2,0,1:T(8,128)(2,1)S(1)} %bitcast.77, bf16[2,512,2048]{2,1,0:T(8,128)(2,1)} %get-tuple-element.5), kind=kOutput, calls=%fused_computation.2 | convolution fusion | flops 2151677952 | bytes 9437184 | tf_op jit(solution)/shard_map/bth,sbkt->bhsk/dot_general | solution.py:76
  99.3 7.8 %reshape_reshape.3 = bf16[2,2,2,2,2,128,512]{5,4,3,2,1,6,0:T(2,128)(2,1)} reshape(bf16[2,2048,16,32]{1,3,2,0:T(8,128)(2,1)} %multiply_convert_fusion) | data formatting | bytes 8388608 | tf_op jit(solution)/shard_map/reshape;reshape | solution.py:21
  107.0 11.5 %constant_dynamic-slice_fusion.4 = (bf16[2,2,2,2,1,128,512]{5,4,3,2,1,6,0:T(2,128)(2,1)}, bf16[2,2,2,2,1,128,512]{5,4,3,2,1,6,0:T(2,128)(2,1)}) fusion(bf16[2,2,2,2,2,128,512]{5,4,3,2,1,6,0:T(2,128)(2,1)} %reshape_reshape.3, s32[]{:T(128)S(6)} %select_n.54, s32[]{:T(128)S(6)} %select_n.55), kind=kLoop, calls=%fused_computation.38 | loop fusion | bytes 8388616 | tf_op jit(solution)/shard_map/jit(dynamic_index_in_dim)/dynamic_slice | solution.py:31
  118.5 10.5 %copy.85 = bf16[2,2,2,2,1,128,512]{6,5,0,4,3,2,1:T(8,128)(2,1)} copy(bf16[2,2,2,2,1,128,512]{5,4,3,2,1,6,0:T(2,128)(2,1)} %get-tuple-element.11) | data formatting | bytes 4194304
  129.5 7.4 %fusion.18 = f32[2,512,512]{2,1,0:T(8,128)} fusion(bf16[2,512,2048]{2,1,0:T(8,128)(2,1)} %get-tuple-element.6, bf16[2,512,2048]{2,1,0:T(8,128)(2,1)} %param.9), kind=kOutput, calls=%fused_computation.50 | convolution fusion | flops 2147483648 | bytes 10485760 | tf_op jit(solution)/shard_map/bth,bih->bit/dot_general | solution.py:109
  136.9 4.2 %add_convert_fusion = bf16[4,2,2,2,1,32,2048]{6,5,0,4,3,2,1:T(8,128)(2,1)S(1)} fusion(bf16[4,2,2,2,1,32,2048]{6,5,0,4,3,2,1:T(8,128)(2,1)} %collective-permute-done, bf16[4,2,2,2,1,32,2048]{6,5,4,3,2,1,0:T(8,128)(2,1)S(1)} %copy-done.1), kind=kLoop, calls=%fused_computation.3 | loop fusion | flops 8388608 | bytes 12582912 | tf_op jit(solution)/shard_map/convert_element_type | solution.py:35
  141.2 1.5 constant_dynamic-slice_fusion.7
  142.6 1.6 collective-permute-start.1
  144.2 1.3 copy-done.4
  145.6 3.7 %fusion.16 = f32[2,512,512]{1,2,0} fusion(bf16[2,512,2048]{2,1,0:T(8,128)(2,1)S(1)} %copy-done.13, bf16[2,2048,512]{2,1,0:T(8,128)(2,1)S(1)} %copy-done.4), kind=kOutput, calls=%fused_computation.48 | convolution fusion | flops 2147483648 | bytes 10485760
  149.2 9.0 %copy.84 = bf16[2,2,2,2,1,128,512]{6,5,0,4,3,2,1:T(8,128)(2,1)S(1)} copy(bf16[2,2,2,2,1,128,512]{5,4,3,2,1,6,0:T(2,128)(2,1)} %get-tuple-element.10) | data formatting | bytes 4194304
  158.3 8.0 %fusion.8 = bf16[2,512,512]{2,1,0:T(8,128)(2,1)} fusion(s32[2,512]{1,0:T(2,128)S(1)} %copy-done.11, f32[2,512,512]{2,1,0:T(8,128)} %fusion.18, bf16[2,512,2048]{2,1,0:T(8,128)(2,1)} %get-tuple-element.7, bf16[2,512,2048]{2,1,0:T(8,128)(2,1)} %param.10), kind=kOutput, calls=%fused_computation.25 | convolution fusion | flops 2686976000 | bytes 11538432 | tf_op jit(solution)/shard_map/bij,bit->bjt/dot_general | solution.py:114
  166.2 2.4 add_convert_fusion.1
  168.7 1.7 collective-permute-start.5
  170.9 1.6 copy.70
  172.5 4.6 %all-to-all-start.1 = ((bf16[2,16,2,32,512]{4,3,2,0,1:T(8,128)(2,1)}), bf16[2,16,2,32,512]{4,3,2,0,1:T(8,128)(2,1)}, u32[]{:S(2)}, u32[]{:S(2)}) async-start(bf16[2,16,2,32,512]{4,3,2,0,1:T(8,128)(2,1)} %copy.70), calls=%async_computation.1 | async-start | bytes 4194304 | tf_op jit(solution)/shard_map/all_to_all | solution.py:120
  177.2 14.3 %collective-permute-done.1 = bf16[4,2,1,2,1,32,2048]{6,5,0,4,3,2,1:T(8,128)(2,1)} collective-permute-done((bf16[4,2,1,2,1,32,2048]{6,5,0,4,3,2,1:T(8,128)(2,1)}, bf16[4,2,1,2,1,32,2048]{6,5,0,4,3,2,1:T(8,128)(2,1)}, u32[]{:S(2)}, u32[]{:S(2)}) %collective-permute-start.1) | collective-permute-done | bytes 2097184 | tf_op jit(solution)/shard_map/ppermute | solution.py:33
  191.4 3.0 %add_convert_fusion.2 = bf16[4,2,1,2,1,32,2048]{6,5,0,4,3,2,1:T(8,128)(2,1)S(1)} fusion(bf16[4,2,1,2,1,32,2048]{6,5,0,4,3,2,1:T(8,128)(2,1)} %collective-permute-done.1, bf16[4,2,2,2,1,32,2048]{6,5,0,4,3,2,1:T(8,128)(2,1)} %copy-done, s32[]{:T(128)S(6)} %select_n.57), kind=kLoop, calls=%fused_computation.14 | loop fusion | flops 4194304 | bytes 6291460 | tf_op jit(solution)/shard_map/convert_element_type | solution.py:35
  194.4 1.0 constant_dynamic-slice_fusion.6
  195.5 3.6 %collective-permute-start.2 = (bf16[4,2,1,1,1,32,2048]{6,5,0,4,3,2,1:T(8,128)(2,1)}, bf16[4,2,1,1,1,32,2048]{6,5,0,4,3,2,1:T(8,128)(2,1)}, u32[]{:S(2)}, u32[]{:S(2)}) collective-permute-start(bf16[4,2,1,1,1,32,2048]{6,5,0,4,3,2,1:T(8,128)(2,1)} %constant_dynamic-slice_fusion.6), channel_id=1, source_target_pairs={{0,16},{16,0},{1,17},{17,1},{2,18},{18,2},{3,19},{19,3},{4,20},{20... | collective-permute-start | bytes 3145736 | tf_op jit(solution)/shard_map/ppermute | solution.py:33
  199.1 13.8 %collective-permute-done.5 = bf16[2,2,1,2,1,128,512]{6,5,0,4,3,2,1:T(8,128)(2,1)} collective-permute-done((bf16[2,2,1,2,1,128,512]{6,5,0,4,3,2,1:T(8,128)(2,1)S(1)}, bf16[2,2,1,2,1,128,512]{6,5,0,4,3,2,1:T(8,128)(2,1)}, u32[]{:S(2)}, u32[]{:S(2)}) %collective-permute-start.5) | collective-permute-done | bytes 1048608 | tf_op jit(solution)/shard_map/ppermute | solution.py:33
  212.8 1.5 add_convert_fusion.3
  214.4 0.8 constant_dynamic-slice_fusion.1
  215.2 3.6 %collective-permute-start.6 = (bf16[2,2,1,1,1,128,512]{6,5,0,4,3,2,1:T(8,128)(2,1)}, bf16[2,2,1,1,1,128,512]{6,5,0,4,3,2,1:T(8,128)(2,1)}, u32[]{:S(2)}, u32[]{:S(2)}) collective-permute-start(bf16[2,2,1,1,1,128,512]{6,5,0,4,3,2,1:T(8,128)(2,1)} %constant_dynamic-slice_fusion.1), channel_id=1, source_target_pairs={{0,16},{16,0},{1,17},{17,1},{2,18},{18,2},{3,19},{19,3},{4,20},{20... | collective-permute-start | bytes 1572872 | tf_op jit(solution)/shard_map/ppermute | solution.py:33
  218.8 19.1 %collective-permute-done.6 = bf16[2,2,1,1,1,128,512]{6,5,0,4,3,2,1:T(8,128)(2,1)} collective-permute-done((bf16[2,2,1,1,1,128,512]{6,5,0,4,3,2,1:T(8,128)(2,1)}, bf16[2,2,1,1,1,128,512]{6,5,0,4,3,2,1:T(8,128)(2,1)}, u32[]{:S(2)}, u32[]{:S(2)}) %collective-permute-start.6) | collective-permute-done | bytes 524320 | tf_op jit(solution)/shard_map/ppermute | solution.py:33
  237.9 1.2 add_convert_fusion.5
  239.1 3.3 %collective-permute-start.7 = (bf16[2,1,1,1,1,128,512]{6,5,0,4,3,2,1:T(8,128)(2,1)S(1)}, bf16[2,1,1,1,1,128,512]{6,5,0,4,3,2,1:T(8,128)(2,1)}, u32[]{:S(2)}, u32[]{:S(2)}) collective-permute-start(bf16[2,1,1,1,1,128,512]{6,5,0,4,3,2,1:T(8,128)(2,1)S(1)} %constant_dynamic-slice_fusion), channel_id=1, source_target_pairs={{0,64},{32,96},{64,0},{96,32},{1,65},{33,97},{65,1},{97,33},{2,66}... | collective-permute-start | bytes 786440 | tf_op jit(solution)/shard_map/ppermute | solution.py:33
  242.4 1.6 add_convert_fusion.4
  244.8 1.8 fusion.13
  246.7 1.1 copy.71
  247.7 1.1 copy.72
  249.1 1.8 add_bitcast_fusion
  250.9 7.8 %collective-permute-done.3 = bf16[4,1,1,1,1,32,2048]{6,5,0,4,3,2,1:T(8,128)(2,1)S(1)} collective-permute-done((bf16[4,1,1,1,1,32,2048]{6,5,0,4,3,2,1:T(8,128)(2,1)S(1)}, bf16[4,1,1,1,1,32,2048]{6,5,0,4,3,2,1:T(8,128)(2,1)S(1)}, u32[]{:S(2)}, u32[]{:S(2)}) %collective-permute-start.3) | collective-permute-done | bytes 524320 | tf_op jit(solution)/shard_map/ppermute | solution.py:33
  258.8 1.1 slice_bitcast_fusion
  (46 shorter events, 4.2 us)
Async XLA Ops:
  4.0 37.0 %all-to-all-start = ((bf16[2,2,16,32,512]{4,3,1,0,2:T(8,128)(2,1)}), bf16[2,2,16,32,512]{4,3,1,0,2:T(8,128)(2,1)S(1)}, u32[]{:S(2)}, u32[]{:S(2)}) async-start(bf16[2,2,16,32,512]{4,3,1,0,2:T(8,128)(2,1)} %copy.61), calls=%async_computation | async-start | bytes 4194304 | tf_op jit(solution)/shard_map/all_to_all | solution.py:52
  41.4 0.7 copy-start.11
  41.4 2.2 copy-start.6
  43.6 2.4 copy-start.5
  65.1 6.7 %copy-start.12 = (bf16[2,512,2048]{2,1,0:T(8,128)(2,1)S(1)}, bf16[2,512,2048]{2,1,0:T(8,128)(2,1)}, u32[]{:S(2)}) copy-start(bf16[2,512,2048]{2,1,0:T(8,128)(2,1)} %get-tuple-element.6) | copy-start | bytes 12582916
  92.7 44.2 %collective-permute-start = (bf16[4,2,2,2,1,32,2048]{6,5,0,4,3,2,1:T(8,128)(2,1)}, bf16[4,2,2,2,1,32,2048]{6,5,0,4,3,2,1:T(8,128)(2,1)}, u32[]{:S(2)}, u32[]{:S(2)}) collective-permute-start(bf16[4,2,2,2,1,32,2048]{6,5,0,4,3,2,1:T(8,128)(2,1)} %copy.83), channel_id=1, source_target_pairs={{0,8},{8,0},{1,9},{9,1},{2,10},{10,2},{3,11},{11,3},{4,12},{12,4},... | collective-permute-start | bytes 12582920 | tf_op jit(solution)/shard_map/ppermute | solution.py:33
  129.0 7.9 %copy-start.1 = (bf16[4,2,2,2,1,32,2048]{6,5,4,3,2,1,0:T(8,128)(2,1)S(1)}, bf16[4,2,2,2,1,32,2048]{6,5,4,3,2,1,0:T(8,128)(2,1)}, u32[]{:S(2)}) copy-start(bf16[4,2,2,2,1,32,2048]{6,5,4,3,2,1,0:T(8,128)(2,1)} %get-tuple-element.8) | copy-start | bytes 12582916
  129.0 37.2 %collective-permute-start.4 = (bf16[2,2,2,2,1,128,512]{6,5,0,4,3,2,1:T(8,128)(2,1)}, bf16[2,2,2,2,1,128,512]{6,5,0,4,3,2,1:T(8,128)(2,1)}, u32[]{:S(2)}, u32[]{:S(2)}) collective-permute-start(bf16[2,2,2,2,1,128,512]{6,5,0,4,3,2,1:T(8,128)(2,1)} %copy.85), channel_id=1, source_target_pairs={{0,8},{8,0},{1,9},{9,1},{2,10},{10,2},{3,11},{11,3},{4,12},{12,4},... | collective-permute-start | bytes 6291464 | tf_op jit(solution)/shard_map/ppermute | solution.py:33
  136.9 7.3 %copy-start.13 = (bf16[2,512,2048]{2,1,0:T(8,128)(2,1)S(1)}, bf16[2,512,2048]{2,1,0:T(8,128)(2,1)}, u32[]{:S(2)}) copy-start(bf16[2,512,2048]{2,1,0:T(8,128)(2,1)} %get-tuple-element.5) | copy-start | bytes 12582916
  141.1 8.1 %copy-start = (bf16[4,2,2,2,1,32,2048]{6,5,0,4,3,2,1:T(8,128)(2,1)}, bf16[4,2,2,2,1,32,2048]{6,5,0,4,3,2,1:T(8,128)(2,1)S(1)}, u32[]{:S(2)}) copy-start(bf16[4,2,2,2,1,32,2048]{6,5,0,4,3,2,1:T(8,128)(2,1)S(1)} %add_convert_fusion) | copy-start | bytes 12582916
  141.1 4.4 %copy-start.4 = (bf16[2,2048,512]{2,1,0:T(8,128)(2,1)S(1)}, bf16[2,2048,512]{2,1,0:T(8,128)(2,1)}, u32[]{:S(2)}) copy-start(bf16[2,2048,512]{2,1,0:T(8,128)(2,1)} %param.11) | copy-start | bytes 12582916
  142.6 48.8 %collective-permute-start.1 = (bf16[4,2,1,2,1,32,2048]{6,5,0,4,3,2,1:T(8,128)(2,1)}, bf16[4,2,1,2,1,32,2048]{6,5,0,4,3,2,1:T(8,128)(2,1)}, u32[]{:S(2)}, u32[]{:S(2)}) collective-permute-start(bf16[4,2,1,2,1,32,2048]{6,5,0,4,3,2,1:T(8,128)(2,1)} %constant_dynamic-slice_fusion.7), channel_id=1, source_target_pairs={{0,32},{32,0},{64,96},{96,64},{1,33},{33,1},{65,97},{97,65},{2,34}... | collective-permute-start | bytes 6291464 | tf_op jit(solution)/shard_map/ppermute | solution.py:33
  166.2 4.2 %copy-start.7 = (f32[2,512,512]{1,2,0:S(1)}, f32[2,512,512]{1,2,0}, u32[]{:S(2)}) copy-start(f32[2,512,512]{1,2,0} %fusion.16) | copy-start | bytes 6291460
  168.6 2.3 copy-start.2
  168.6 2.1 copy-start.10
  168.7 44.1 %collective-permute-start.5 = (bf16[2,2,1,2,1,128,512]{6,5,0,4,3,2,1:T(8,128)(2,1)S(1)}, bf16[2,2,1,2,1,128,512]{6,5,0,4,3,2,1:T(8,128)(2,1)}, u32[]{:S(2)}, u32[]{:S(2)}) collective-permute-start(bf16[2,2,1,2,1,128,512]{6,5,0,4,3,2,1:T(8,128)(2,1)S(1)} %constant_dynamic-slice_fusion.2), channel_id=1, source_target_pairs={{0,32},{32,0},{64,96},{96,64},{1,33},{33,1},{65,97},{97,65},{2,34}... | collective-permute-start | bytes 3145736 | tf_op jit(solution)/shard_map/ppermute | solution.py:33
  172.5 72.3 %all-to-all-start.1 = ((bf16[2,16,2,32,512]{4,3,2,0,1:T(8,128)(2,1)}), bf16[2,16,2,32,512]{4,3,2,0,1:T(8,128)(2,1)}, u32[]{:S(2)}, u32[]{:S(2)}) async-start(bf16[2,16,2,32,512]{4,3,2,0,1:T(8,128)(2,1)} %copy.70), calls=%async_computation.1 | async-start | bytes 4194304 | tf_op jit(solution)/shard_map/all_to_all | solution.py:120
  177.2 35.7 %copy-start.3 = (bf16[2,2,2,2,1,128,512]{6,5,0,4,3,2,1:T(8,128)(2,1)S(1)}, bf16[2,2,2,2,1,128,512]{6,5,0,4,3,2,1:T(8,128)(2,1)}, u32[]{:S(2)}) copy-start(bf16[2,2,2,2,1,128,512]{6,5,0,4,3,2,1:T(8,128)(2,1)} %copy-done.2) | copy-start | bytes 6291460
  195.5 46.9 %collective-permute-start.2 = (bf16[4,2,1,1,1,32,2048]{6,5,0,4,3,2,1:T(8,128)(2,1)}, bf16[4,2,1,1,1,32,2048]{6,5,0,4,3,2,1:T(8,128)(2,1)}, u32[]{:S(2)}, u32[]{:S(2)}) collective-permute-start(bf16[4,2,1,1,1,32,2048]{6,5,0,4,3,2,1:T(8,128)(2,1)} %constant_dynamic-slice_fusion.6), channel_id=1, source_target_pairs={{0,16},{16,0},{1,17},{17,1},{2,18},{18,2},{3,19},{19,3},{4,20},{20... | collective-permute-start | bytes 3145736 | tf_op jit(solution)/shard_map/ppermute | solution.py:33
  215.2 22.7 %collective-permute-start.6 = (bf16[2,2,1,1,1,128,512]{6,5,0,4,3,2,1:T(8,128)(2,1)}, bf16[2,2,1,1,1,128,512]{6,5,0,4,3,2,1:T(8,128)(2,1)}, u32[]{:S(2)}, u32[]{:S(2)}) collective-permute-start(bf16[2,2,1,1,1,128,512]{6,5,0,4,3,2,1:T(8,128)(2,1)} %constant_dynamic-slice_fusion.1), channel_id=1, source_target_pairs={{0,16},{16,0},{1,17},{17,1},{2,18},{18,2},{3,19},{19,3},{4,20},{20... | collective-permute-start | bytes 1572872 | tf_op jit(solution)/shard_map/ppermute | solution.py:33
  239.1 3.3 %copy-start.8 = (bf16[2,2,1,1,1,128,512]{6,5,0,4,3,2,1:T(8,128)(2,1)}, bf16[2,2,1,1,1,128,512]{6,5,0,4,3,2,1:T(8,128)(2,1)S(1)}, u32[]{:S(2)}) copy-start(bf16[2,2,1,1,1,128,512]{6,5,0,4,3,2,1:T(8,128)(2,1)S(1)} %add_convert_fusion.5) | copy-start | bytes 1572868
  239.1 10.0 %collective-permute-start.7 = (bf16[2,1,1,1,1,128,512]{6,5,0,4,3,2,1:T(8,128)(2,1)S(1)}, bf16[2,1,1,1,1,128,512]{6,5,0,4,3,2,1:T(8,128)(2,1)}, u32[]{:S(2)}, u32[]{:S(2)}) collective-permute-start(bf16[2,1,1,1,1,128,512]{6,5,0,4,3,2,1:T(8,128)(2,1)S(1)} %constant_dynamic-slice_fusion), channel_id=1, source_target_pairs={{0,64},{32,96},{64,0},{96,32},{1,65},{33,97},{65,1},{97,33},{2,66}... | collective-permute-start | bytes 786440 | tf_op jit(solution)/shard_map/ppermute | solution.py:33
  244.1 14.6 %collective-permute-start.3 = (bf16[4,1,1,1,1,32,2048]{6,5,0,4,3,2,1:T(8,128)(2,1)S(1)}, bf16[4,1,1,1,1,32,2048]{6,5,0,4,3,2,1:T(8,128)(2,1)S(1)}, u32[]{:S(2)}, u32[]{:S(2)}) collective-permute-start(bf16[4,1,1,1,1,32,2048]{6,5,0,4,3,2,1:T(8,128)(2,1)S(1)} %constant_dynamic-slice_fusion.5), channel_id=1, source_target_pairs={{0,64},{32,96},{64,0},{96,32},{1,65},{33,97},{65,1},{97,33},{2,66}... | collective-permute-start | bytes 1572872 | tf_op jit(solution)/shard_map/ppermute | solution.py:33
  244.8 4.3 %copy-start.9 = (bf16[2,2,1,1,1,128,512]{6,5,0,4,3,2,1:T(8,128)(2,1)S(1)}, bf16[2,2,1,1,1,128,512]{6,5,0,4,3,2,1:T(8,128)(2,1)}, u32[]{:S(2)}) copy-start(bf16[2,2,1,1,1,128,512]{6,5,0,4,3,2,1:T(8,128)(2,1)} %copy-done.8) | copy-start | bytes 1572868
